TPU v7x, 128 devices: a whole 4x4x4 slice. The times are simulated.
128 devices in a mesh: section: 4 (over x), sample: 8 (over z, y_lo), tensor: 4 (over y_hi, core).
Axes of the slice: x: 4, y: 4 (y_hi: 2, y_lo: 2; y = y_hi * 2 + y_lo), z: 4, core: 2. Of those that a mesh axis runs over, the one named last changes fastest.
Arguments:
- queries: bfloat16 [4, 1024, 8192], P('section', 'sample', 'tensor'), may hold values from -4.5 to 4.5
- suffix_keys: bfloat16 [4, 1024, 1024], P('section', 'sample', 'tensor'), may hold values from -4.5 to 4.5
- suffix_values: bfloat16 [4, 1024, 1024], P('section', 'sample', 'tensor'), may hold values from -4.5 to 4.5
- output_grad: bfloat16 [4, 1024, 8192], P('section', 'sample', 'tensor'), may hold values from -192 to 192
- prefix_keys: bfloat16 [4, 4096, 1024], P('section', ('sample', 'tensor')), may hold values from -4.5 to 4.5
- prefix_values: bfloat16 [4, 4096, 1024], P('section', ('sample', 'tensor')), may hold values from -4.5 to 4.5
- kv_weight: bfloat16 [4, 8192, 2, 1024], P('section', None, None, 'tensor'), may hold values from -0.0625 to 0.0625
- prefix_states: bfloat16 [4, 4096, 8192], P('section', ('sample', 'tensor')), may hold values from -6 to 6
- norm_gain: bfloat16 [4, 8192], P('section'), may hold values from 0.099609375 to 1.8984375
- segment_ids: int32 [8, 128], P('sample'), may hold values from 0 to 1, never falling along the last dimension, each value on 1 to 96 neighbouring positions
- segment_prompt: int32 [8, 2], P('sample'), may hold values from 0 to 2
- block_table: int32 [3, 16], replicated, may hold values from 0 to 31, as said below
Outputs:
- query_grad: bfloat16 [4, 1024, 8192], P('section', 'sample', 'tensor')
- rollout_key_gradient: bfloat16 [4, 1024, 1024], P('section', 'sample', 'tensor')
- suffix_value_grad: bfloat16 [4, 1024, 1024], P('section', 'sample', 'tensor')
- prefix_key_grad: float32 [4, 4096, 1024], P('section', ('sample', 'tensor'))
- prefix_value_grad: float32 [4, 4096, 1024], P('section', ('sample', 'tensor'))
- prefix_state_gradient: float32 [4, 4096, 8192], P('section', ('sample', 'tensor'))
Inputs may be any that keep to these rules, and one draw needn't show every extreme that they name: `block_table`: each row lists 16 distinct pages; its first 8 entries are the same pages in every row, and every page of the pool appears in some row.
All inputs are finite; a program needn't handle non-finite values.
Results may differ from a plain program's by a relative error of at most 0.024.
Values may be sent and summed in bfloat16 or wider, within the bound.
No kernel may reach another device: no remote copies, remote signals or barrier semaphores. Data moves between devices by JAX's collectives and lax.ppermute only.
A program may use at most 192 MiB of HBM per device.

v0:
```python
import jax
import jax.numpy as jnp
from jax import lax
from jax.sharding import PartitionSpec as P

HEAD_SIZE = 128
PAGE = 128


MASKED_SCORE = -1e30
EPSILON = 1e-05


def entering(value, axis, join, neutral):
    count = lax.axis_size(axis)
    place = lax.axis_index(axis)
    ahead = count - 1 - place
    gathered = lax.all_gather(value.astype(jnp.bfloat16), axis)
    state = jnp.zeros_like(value) + jnp.asarray(neutral, value.dtype)

    def one(turn, state):
        source = count - 1 - turn
        return join(state, lax.dynamic_index_in_dim(gathered, source, 0, False).astype(value.dtype))

    return lax.fori_loop(0, ahead, one, state)


def visible_keys(seg_row, prompt_row, table, pooled_rows):
    tok_count = seg_row.shape[0]
    seg_hot = seg_row[:, None] == jnp.arange(prompt_row.shape[0], dtype=jnp.int32)[None, :]
    prompt_tok = jnp.sum(jnp.where(seg_hot, prompt_row[None, :], 0), axis=1)
    page_ids = jnp.arange(pooled_rows // PAGE, dtype=jnp.int32)
    member = jnp.any(table[:, :, None] == page_ids[None, None, :], axis=1)
    prompt_hot = prompt_tok[:, None] == jnp.arange(table.shape[0], dtype=jnp.int32)[None, :]
    member_tok = jnp.any(prompt_hot[:, :, None] & member[None, :, :], axis=1)
    prefix_seen = jnp.repeat(member_tok, PAGE, axis=1)
    position = jnp.arange(tok_count, dtype=jnp.int32)
    suffix_seen = (seg_row[:, None] == seg_row[None, :]) & (position[None, :] <= position[:, None])
    return jnp.concatenate([prefix_seen, suffix_seen], axis=1)


def attend_group(query_grp, grad_grp, key_rows, value_rows, visible):
    inv_root = query_grp.shape[-1] ** (-0.5)
    scores = (
        jnp.einsum("rgd,kd->rgk", query_grp, key_rows, preferred_element_type=jnp.float32)
        * inv_root
    )
    scores = jnp.where(visible[:, None, :], scores, MASKED_SCORE)
    row_max = jnp.max(scores, axis=2, keepdims=True)
    exponent = jnp.exp(scores - row_max)
    softmax_w = exponent / jnp.sum(exponent, axis=2, keepdims=True)
    weights_low = softmax_w.astype(jnp.bfloat16)
    attended = jnp.einsum(
        "rgk,kd->rgd", weights_low, value_rows, preferred_element_type=jnp.float32
    )
    delta_row = jnp.sum(grad_grp.astype(jnp.float32) * attended, axis=2, keepdims=True)
    weight_grad = jnp.einsum(
        "rgd,kd->rgk", grad_grp, value_rows, preferred_element_type=jnp.float32
    )
    score_grad = (softmax_w * (weight_grad - delta_row)).astype(jnp.bfloat16)
    query_out = (
        jnp.einsum("rgk,kd->rgd", score_grad, key_rows, preferred_element_type=jnp.float32)
        * inv_root
    )
    key_result = (
        jnp.einsum("rgk,rgd->kd", score_grad, query_grp, preferred_element_type=jnp.float32)
        * inv_root
    )
    value_out = jnp.einsum("rgk,rgd->kd", weights_low, grad_grp, preferred_element_type=jnp.float32)
    return (query_out, key_result, value_out)


def add_terms(earlier, later_term):
    return earlier + later_term


def on_device(
    queries,
    suffix_keys,
    suffix_values,
    output_grad,
    prefix_keys,
    prefix_values,
    kv_weight,
    prefix_states,
    norm_gain,
    segment_ids,
    segment_prompt,
    block_table,
):
    head_width = suffix_keys.shape[2]
    key_store, value_store = (
        lax.all_gather(prefix_keys, ("sample", "tensor"), axis=1, tiled=True),
        lax.all_gather(prefix_values, ("sample", "tensor"), axis=1, tiled=True),
    )
    offset = lax.axis_index("tensor") * head_width
    key_pool = lax.dynamic_slice_in_dim(key_store, offset, head_width, 2)[0]
    value_pool = lax.dynamic_slice_in_dim(value_store, offset, head_width, 2)[0]
    pooled_rows = key_pool.shape[0]
    tok_count = queries.shape[1]
    kv_local = head_width // HEAD_SIZE
    group_size = queries.shape[2] // head_width
    visible = visible_keys(segment_ids[0], segment_prompt[0], block_table, pooled_rows)
    query_rows = queries[0].reshape(tok_count, kv_local, group_size, HEAD_SIZE)
    grad_rows = output_grad[0].reshape(tok_count, kv_local, group_size, HEAD_SIZE)
    own_keys = suffix_keys[0]
    own_values = suffix_values[0]
    query_pieces, suffix_key_pieces, suffix_value_pieces, prefix_key_pieces, prefix_value_pieces = (
        [],
        [],
        [],
        [],
        [],
    )
    for head_index in range(kv_local):
        low_col = head_index * HEAD_SIZE
        key_rows = jnp.concatenate(
            [
                key_pool[:, low_col : low_col + HEAD_SIZE],
                own_keys[:, low_col : low_col + HEAD_SIZE],
            ],
            axis=0,
        )
        value_rows = jnp.concatenate(
            [
                value_pool[:, low_col : low_col + HEAD_SIZE],
                own_values[:, low_col : low_col + HEAD_SIZE],
            ],
            axis=0,
        )
        query_out, key_result, value_out = attend_group(
            query_rows[:, head_index], grad_rows[:, head_index], key_rows, value_rows, visible
        )
        query_pieces.append(query_out)
        prefix_key_pieces.append(key_result[:pooled_rows])
        suffix_key_pieces.append(key_result[pooled_rows:])
        prefix_value_pieces.append(value_out[:pooled_rows])
        suffix_value_pieces.append(value_out[pooled_rows:])
    query_grad = jnp.stack(query_pieces, axis=1).reshape(tok_count, -1).astype(jnp.bfloat16)
    rollout_key_gradient = jnp.concatenate(suffix_key_pieces, axis=1).astype(jnp.bfloat16)
    suffix_value_grad = jnp.concatenate(suffix_value_pieces, axis=1).astype(jnp.bfloat16)
    pooled_key = jnp.concatenate(prefix_key_pieces, axis=1)
    pooled_value = jnp.concatenate(prefix_value_pieces, axis=1)
    key_reduced, value_reduced = (
        lax.psum_scatter(
            pooled_key.astype(jnp.bfloat16), "sample", scatter_dimension=0, tiled=True
        ).astype(jnp.float32),
        lax.psum_scatter(
            pooled_value.astype(jnp.bfloat16), "sample", scatter_dimension=0, tiled=True
        ).astype(jnp.float32),
    )
    key_home, value_home = (
        lax.all_to_all(
            key_reduced.astype(jnp.bfloat16), "tensor", split_axis=0, concat_axis=1, tiled=True
        ).astype(key_reduced.dtype),
        lax.all_to_all(
            value_reduced.astype(jnp.bfloat16), "tensor", split_axis=0, concat_axis=1, tiled=True
        ).astype(value_reduced.dtype),
    )
    stacked = jnp.stack(
        [key_reduced.astype(jnp.bfloat16), value_reduced.astype(jnp.bfloat16)], axis=1
    )
    weight_local = kv_weight[0]
    normed_grad = lax.psum_scatter(
        lax.dot_general(
            stacked, weight_local, (((1, 2), (1, 2)), ((), ())), preferred_element_type=jnp.float32
        ).astype(jnp.bfloat16),
        "tensor",
        scatter_dimension=0,
        tiled=True,
    ).astype(jnp.float32)
    states = prefix_states[0].astype(jnp.float32)
    gain_wide = norm_gain[0].astype(jnp.float32)[None, :]
    inv_rms = lax.rsqrt(jnp.mean(states * states, axis=1, keepdims=True) + EPSILON)
    gained = gain_wide * normed_grad
    layer_term = inv_rms * gained - states * inv_rms**3 * jnp.mean(
        states * gained, axis=1, keepdims=True
    )
    higher_terms = entering(layer_term, "section", add_terms, jnp.zeros_like(layer_term))
    prefix_state_gradient = higher_terms + layer_term
    return (
        query_grad[None],
        rollout_key_gradient[None],
        suffix_value_grad[None],
        key_home[None],
        value_home[None],
        prefix_state_gradient[None],
    )


def solution(mesh):
    placed = (
        P("section", "sample", "tensor"),
        P("section", "sample", "tensor"),
        P("section", "sample", "tensor"),
        P("section", "sample", "tensor"),
        P("section", ("sample", "tensor"), None),
        P("section", ("sample", "tensor"), None),
        P("section", None, None, "tensor"),
        P("section", ("sample", "tensor"), None),
        P("section", None),
        P("sample", None),
        P("sample", None),
        P(),
    )
    return jax.shard_map(
        on_device,
        mesh=mesh,
        in_specs=placed,
        out_specs=(
            P("section", "sample", "tensor"),
            P("section", "sample", "tensor"),
            P("section", "sample", "tensor"),
            P("section", ("sample", "tensor"), None),
            P("section", ("sample", "tensor"), None),
            P("section", ("sample", "tensor"), None),
        ),
        check_vma=False,
    )
```

profile of v0, /device:TPU:0, one launch (start us, length us, event | category | flops | bytes accessed | tf_op | source)
XLA Modules:
  0.0 551.7 jit_solution(3952926247144493262)
XLA Ops:
  7.3 0.7 all-gather.5.cloned.1.call-update
  8.0 0.7 all-gather.7.cloned.1.call-update
  8.8 2.0 copy.107
  10.8 1.3 copy.109
  12.2 0.9 copy.164
  13.0 0.2 copy.166
  13.8 64.6 %all-gather.5.cloned.1.call-done = bf16[1,4096,1024]{2,1,0:T(8,128)(2,1)} async-done(((bf16[1,128,1024]{2,1,0:T(8,128)(2,1)}), bf16[1,4096,1024]{2,1,0:T(8,128)(2,1)}) %all-gather.5.cloned.1.call-update) | async-done | bytes 8388624 | tf_op jit(solution)/shard_map/all_gather | solution.py:93
  78.5 67.3 %all-gather.7.cloned.1.call-done = bf16[1,4096,1024]{2,1,0:T(8,128)(2,1)} async-done(((bf16[1,128,1024]{2,1,0:T(8,128)(2,1)}), bf16[1,4096,1024]{2,1,0:T(8,128)(2,1)}) %all-gather.7.cloned.1.call-update) | async-done | bytes 8388624 | tf_op jit(solution)/shard_map/all_gather | solution.py:94
  145.7 2.5 dynamic-slice_bitcast_fusion
  148.3 1.5 fusion.61
  149.9 1.0 copy-done.4
  150.9 2.4 fusion.33
  153.3 10.7 %fusion.67 = (f32[128,8]{0,1:T(8,128)S(1)}, f32[128,8,4224]{0,2,1:T(8,128)}) fusion(f32[4224,128,8]{1,0,2:T(8,128)S(1)} %fusion.33, pred[128,4224]{0,1:T(8,128)(4,1)S(1)} %pad_add_fusion), kind=kOutput, calls=%fused_computation.118 | output fusion | flops 17305728 | bytes 35147776 | tf_op jit(solution)/shard_map/sub | solution.py:50
  164.0 7.5 %fusion.13 = bf16[128,8,4224]{0,2,1:T(8,128)(2,1)S(1)} fusion(f32[128,8,4224]{0,2,1:T(8,128)} %get-tuple-element.112, f32[128,8]{0,1:T(8,128)S(1)} %get-tuple-element.111), kind=kLoop, calls=%fused_computation.23 | loop fusion | flops 8650752 | bytes 25956352 | tf_op jit(solution)/shard_map/convert_element_type | solution.py:52
  171.5 4.4 copy-done.2
  175.8 2.5 fusion.28
  178.5 7.1 %fusion.3 = bf16[128,8,4224]{0,2,1:T(8,128)(2,1)} fusion(f32[128,8]{0,1:T(8,128)S(1)} %fusion.28, f32[128,8,4224]{0,2,1:T(8,128)S(1)} %bitcast.161, f32[128,8]{0,1:T(8,128)S(1)} %get-tuple-element.111, bf16[128,128]{1,0:T(8,128)(2,1)S(1)} %get-tuple-element.103, bf16[4096,128]{1,0:T(8,128)(2,1)} %get-tuple-element.97, bf16[128,2,8,128]{0,3,2,1:T(8,128)(2,1)} %bitcast.168), kind=kOutput, calls=%fused_computation.7 | convolution fusion | flops 1126760448 | bytes 27303936 | tf_op jit(solution)/shard_map/rgd,kd->rgk/dot_general | solution.py:57
  185.7 6.4 %fusion.17 = bf16[4224,128]{0,1:T(8,128)(2,1)S(1)} fusion(bf16[128,8,4224]{0,2,1:T(8,128)(2,1)} %fusion.3, bf16[128,2,8,128]{0,3,2,1:T(8,128)(2,1)} %bitcast.163), kind=kOutput, calls=%fused_computation.34 | convolution fusion | flops 1108377600 | bytes 9994240 | tf_op jit(solution)/shard_map/rgk,rgd->kd/dot_general | solution.py:66
  192.1 1.0 copy-done.5
  193.0 2.4 fusion.32
  195.4 10.2 %fusion.66 = (f32[128,8]{0,1:T(8,128)S(1)}, f32[128,8,4224]{0,2,1:T(8,128)}) fusion(f32[4224,128,8]{1,0,2:T(8,128)S(1)} %fusion.32, pred[128,4224]{0,1:T(8,128)(4,1)S(1)} %pad_add_fusion), kind=kOutput, calls=%fused_computation.117 | output fusion | flops 17305728 | bytes 35147776 | tf_op jit(solution)/shard_map/sub | solution.py:50
  205.7 7.5 %fusion.14 = bf16[128,8,4224]{0,2,1:T(8,128)(2,1)S(1)} fusion(f32[128,8,4224]{0,2,1:T(8,128)} %get-tuple-element.110, f32[128,8]{0,1:T(8,128)S(1)} %get-tuple-element.109), kind=kLoop, calls=%fused_computation.24 | loop fusion | flops 8650752 | bytes 25956352 | tf_op jit(solution)/shard_map/convert_element_type | solution.py:52
  213.1 4.4 copy-done.3
  217.5 2.5 fusion.29
  220.2 7.2 %fusion.2 = bf16[128,8,4224]{0,2,1:T(8,128)(2,1)} fusion(f32[128,8]{0,1:T(8,128)S(1)} %fusion.29, f32[128,8,4224]{0,2,1:T(8,128)S(1)} %bitcast.159, f32[128,8]{0,1:T(8,128)S(1)} %get-tuple-element.109, bf16[128,128]{1,0:T(8,128)(2,1)S(1)} %get-tuple-element.104, bf16[4096,128]{1,0:T(8,128)(2,1)} %get-tuple-element.98, bf16[128,2,8,128]{0,3,2,1:T(8,128)(2,1)} %bitcast.169), kind=kOutput, calls=%fused_computation.4 | convolution fusion | flops 1126760448 | bytes 27303936 | tf_op jit(solution)/shard_map/rgd,kd->rgk/dot_general | solution.py:57
  227.4 6.4 %fusion.18 = bf16[4224,128]{0,1:T(8,128)(2,1)S(1)} fusion(bf16[128,8,4224]{0,2,1:T(8,128)(2,1)} %fusion.2, bf16[128,2,8,128]{0,3,2,1:T(8,128)(2,1)S(1)} %bitcast.166), kind=kOutput, calls=%fused_computation.35 | convolution fusion | flops 1108377600 | bytes 9994240 | tf_op jit(solution)/shard_map/rgk,rgd->kd/dot_general | solution.py:66
  233.8 1.0 copy-done.11
  234.9 1.5 pad_maximum_fusion
  236.5 6.3 %fusion.19 = bf16[4224,128]{0,1:T(8,128)(2,1)S(1)} fusion(bf16[128,8,4224]{0,2,1:T(8,128)(2,1)} %copy-done.2, bf16[128,2,8,128]{0,3,2,1:T(8,128)(2,1)S(1)} %bitcast.170), kind=kOutput, calls=%fused_computation.36 | convolution fusion | flops 1107836928 | bytes 9994240 | tf_op jit(solution)/shard_map/rgk,rgd->kd/dot_general | solution.py:69
  242.9 1.0 copy-done.13
  244.0 6.5 %fusion.20 = bf16[4224,128]{0,1:T(8,128)(2,1)S(1)} fusion(bf16[128,8,4224]{0,2,1:T(8,128)(2,1)} %copy-done.3, bf16[128,2,8,128]{0,3,2,1:T(8,128)(2,1)S(1)} %bitcast.171), kind=kOutput, calls=%fused_computation.37 | convolution fusion | flops 1107836928 | bytes 9994240 | tf_op jit(solution)/shard_map/rgk,rgd->kd/dot_general | solution.py:69
  250.6 1.5 pad_maximum_fusion.1
  252.2 0.3 reduce-scatter.8.cloned.1.call-start
  252.5 36.3 %reduce-scatter.4.cloned.1.call-done = bf16[512,256]{0,1:T(8,128)(2,1)} async-done(((bf16[4096,256]{0,1:T(8,128)(2,1)}), bf16[512,256]{0,1:T(8,128)(2,1)}) %reduce-scatter.4.cloned.1.call-update) | async-done | bytes 262160 | tf_op jit(solution)/shard_map/reduce_scatter | solution.py:145
  288.8 54.1 %reduce-scatter.6.cloned.1.call-done = bf16[512,256]{0,1:T(8,128)(2,1)} async-done(((bf16[4096,256]{0,1:T(8,128)(2,1)}), bf16[512,256]{0,1:T(8,128)(2,1)}) %reduce-scatter.6.cloned.1.call-update) | async-done | bytes 262160 | tf_op jit(solution)/shard_map/reduce_scatter | solution.py:148
  342.9 11.4 %bitcast_convert_fusion = bf16[512,8192]{1,0:T(8,128)(2,1)} fusion(bf16[8192,2,256]{2,1,0:T(2,128)(2,1)} %bitcast.185, bf16[512,1,256]{0,2,1:T(8,128)(2,1)} %bitcast.180, bf16[512,1,256]{0,2,1:T(8,128)(2,1)} %bitcast.179), kind=kOutput, calls=%fused_computation.11 | convolution fusion | flops 4299423744 | bytes 17301504 | tf_op jit(solution)/shard_map/dot_general | solution.py:165
  354.4 0.7 copy-done.22
  355.1 76.7 %reduce-scatter.8.cloned.1.call-done = bf16[128,8192]{1,0:T(8,128)(2,1)} async-done(((bf16[512,8192]{1,0:T(8,128)(2,1)}), bf16[128,8192]{1,0:T(8,128)(2,1)}) %reduce-scatter.8.cloned.1.call-update) | async-done | bytes 2097168 | tf_op jit(solution)/shard_map/reduce_scatter | solution.py:164
  431.9 2.8 fusion.21
  434.7 2.8 fusion.25
  437.6 5.1 fusion.31
  442.7 5.1 fusion.30
  447.9 1.0 copy.135
  448.9 0.8 slice_bitcast_fusion.9
  449.7 0.8 slice_bitcast_fusion.7
  450.4 0.8 slice_bitcast_fusion.8
  451.2 0.8 slice_bitcast_fusion.6
  452.0 1.7 copy_bitcast_fusion
  453.7 3.4 all-to-all-start.1
  457.1 0.7 copy_bitcast_fusion.1
  457.9 6.7 %all-to-all-done.1 = bf16[4,128,256]{1,2,0:T(8,128)(2,1)S(1)} async-done(((bf16[4,128,256]{1,2,0:T(8,128)(2,1)}), bf16[4,128,256]{1,2,0:T(8,128)(2,1)S(1)}, u32[]{:S(2)}, u32[]{:S(2)}) %all-to-all-start.1) | async-done | bytes 262176 | tf_op jit(solution)/shard_map/all_to_all | solution.py:156
  464.6 3.4 all-to-all-start
  468.0 0.7 copy.136
  468.8 0.7 copy.137
  469.6 1.0 copy.139
  470.5 4.9 all-to-all-done
  475.5 1.0 copy.138
  476.5 43.6 %all-gather.9.cloned.1.call-done = bf16[512,8192]{1,0:T(8,128)(2,1)} async-done(((bf16[128,8192]{1,0:T(8,128)(2,1)}), bf16[512,8192]{1,0:T(8,128)(2,1)}) %all-gather.9.cloned.1.call-update) | async-done | bytes 8388624 | tf_op jit(solution)/shard_map/all_gather | solution.py:18
  520.1 2.5 broadcast_in_dim.42
  522.6 15.9 %while.12 = (s32[]{:T(128)}, f32[128,8192]{1,0:T(8,128)}, s32[]{:T(128)}, bf16[4,128,8192]{2,1,0:T(8,128)(2,1)}, s32[]{:T(128)}, /*index=5*/s32[]{:T(128)}, s32[]{:T(128)}, s32[]{:T(128)}) while((s32[]{:T(128)}, f32[128,8192]{1,0:T(8,128)}, s32[]{:T(128)}, bf16[4,128,8192]{2,1,0:T(8,128)(2,1)}, s32[]{:T(128)}, /*index=5*/s32[]{:T(128)}, ...), condition=%wide.region_15.16_spmd, body=%wide.region_14.15_spmd.sunk | while | flops 2097158 | bytes 10485903 | solution.py:25
  522.6 5.3 convert_add_fusion.2
  527.9 5.3 convert_add_fusion.2
  533.2 5.3 convert_add_fusion.2
  538.5 6.1 %add_bitcast_fusion = f32[1,128,8192]{2,1,0:T(8,128)} fusion(f32[128,8192]{1,0:T(8,128)} %get-tuple-element.62, bf16[128,8192]{1,0:T(8,128)(2,1)} %reduce-scatter.8.cloned.1.call-done, bf16[1,128,8192]{2,1,0:T(8,128)(2,1)S(1)} %copy-done, f32[128]{0:T(128)S(1)} %broadcast_multiply_fusion, f32[128]{0:T(128)S(1)} %get-tuple-element.108, ...), kind=kLoop, calls=%fused_computation.42 | loop fusion | flops 8388608 | bytes 12617216 | tf_op jit(solution)/shard_map/broadcast_in_dim | solution.py:187
  (100 shorter events, 1.8 us)
Async XLA Ops:
  7.2 6.0 %copy-start.25 = (s32[1,2]{1,0:T(1,128)S(1)}, s32[1,2]{1,0:T(1,128)}, u32[]{:S(2)}) copy-start(s32[1,2]{1,0:T(1,128)} %param.24) | copy-start | bytes 28
  7.2 6.0 %copy-start.23 = (s32[1,128]{1,0:T(1,128)S(1)}, s32[1,128]{1,0:T(1,128)}, u32[]{:S(2)}) copy-start(s32[1,128]{1,0:T(1,128)} %param.23) | copy-start | bytes 1540
  7.2 6.1 %copy-start.24 = (s32[3,16]{1,0:T(4,128)S(1)}, s32[3,16]{1,0:T(4,128)}, u32[]{:S(2)}) copy-start(s32[3,16]{1,0:T(4,128)} %param.25) | copy-start | bytes 580
  7.2 6.4 %copy-start.20 = (bf16[1,128,256]{2,1,0:T(8,128)(2,1)S(1)}, bf16[1,128,256]{2,1,0:T(8,128)(2,1)}, u32[]{:S(2)}) copy-start(bf16[1,128,256]{2,1,0:T(8,128)(2,1)} %param.15) | copy-start | bytes 196612
  7.2 6.4 %copy-start.21 = (bf16[1,128,256]{2,1,0:T(8,128)(2,1)S(1)}, bf16[1,128,256]{2,1,0:T(8,128)(2,1)}, u32[]{:S(2)}) copy-start(bf16[1,128,256]{2,1,0:T(8,128)(2,1)} %param.16) | copy-start | bytes 196612
  7.2 71.2 %all-gather.5.cloned.1.call-start = ((), (), s32[]{:S(2)}) async-start(), calls=%async_computation.5 | async-start | bytes 8650752 | tf_op jit(solution)/shard_map/all_gather | solution.py:93
  8.0 137.8 %all-gather.7.cloned.1.call-start = ((), (), s32[]{:S(2)}) async-start(), calls=%async_computation.6 | async-start | bytes 8650752 | tf_op jit(solution)/shard_map/all_gather | solution.py:94
  8.7 280.1 %reduce-scatter.4.cloned.1.call-start = ((), (), s32[]{:S(2)}) async-start(), calls=%async_computation.7 | async-start | bytes 2359296 | tf_op jit(solution)/shard_map/reduce_scatter | solution.py:145
  12.1 136.2 %copy-start.9 = (bf16[1,128,2048]{1,2,0:T(8,128)(2,1)}, bf16[1,128,2048]{1,2,0:T(8,128)(2,1)S(1)}, u32[]{:S(2)}) copy-start(bf16[1,128,2048]{1,2,0:T(8,128)(2,1)S(1)} %copy.109) | copy-start | bytes 1572868
  13.6 136.3 %copy-start.18 = (bf16[128,128]{1,0:T(8,128)(2,1)}, bf16[128,128]{1,0:T(8,128)(2,1)S(1)}, u32[]{:S(2)}) copy-start(bf16[128,128]{1,0:T(8,128)(2,1)S(1)} %get-tuple-element.105) | copy-start | bytes 98308
  148.3 2.6 copy-start.6
  149.9 1.0 copy-start.4
  163.9 11.9 %copy-start.15 = (bf16[4096,128]{1,0:T(8,128)(2,1)S(1)}, bf16[4096,128]{1,0:T(8,128)(2,1)}, u32[]{:S(2)}) copy-start(bf16[4096,128]{1,0:T(8,128)(2,1)} %get-tuple-element.97) | copy-start | bytes 3145732
  163.9 11.9 %copy-start.17 = (bf16[128,1,8,128]{3,0,2,1:T(8,128)(2,1)S(1)}, bf16[128,1,8,128]{3,0,2,1:T(8,128)(2,1)}, u32[]{:S(2)}) copy-start(bf16[128,1,8,128]{3,0,2,1:T(8,128)(2,1)} %copy.164) | copy-start | bytes 786436
  163.9 14.4 %slice-start.5 = ((s8[17301504]{0:T(1024)(128)(4,1)}), s8[4194304]{0:T(1024)(128)(4,1)S(1)}, s32[]{:S(2)}) async-start(s8[17301504]{0:T(1024)(128)(4,1)} %bitcast.160), calls=%async_computation.16 | async-start | bytes 8388608
  163.9 14.4 %slice-start.6 = ((s8[17301504]{0:T(1024)(128)(4,1)}), s8[4194304]{0:T(1024)(128)(4,1)S(1)}, s32[]{:S(2)}) async-start(s8[17301504]{0:T(1024)(128)(4,1)} %bitcast.160), calls=%async_computation.17 | async-start | bytes 8388608
  163.9 14.4 %slice-start.7 = ((s8[17301504]{0:T(1024)(128)(4,1)}), s8[4194304]{0:T(1024)(128)(4,1)S(1)}, s32[]{:S(2)}) async-start(s8[17301504]{0:T(1024)(128)(4,1)} %bitcast.160), calls=%async_computation.18 | async-start | bytes 8388608
  164.0 14.4 %slice-start.8 = ((s8[17301504]{0:T(1024)(128)(4,1)}), s8[4194304]{0:T(1024)(128)(4,1)S(1)}, s32[]{:S(2)}) async-start(s8[17301504]{0:T(1024)(128)(4,1)} %bitcast.160), calls=%async_computation.19 | async-start | bytes 8388608
  171.4 4.4 copy-start.2
  175.8 2.7 slice-start.9
  185.6 7.4 %copy-start.7 = (bf16[1,128,2048]{1,2,0:T(8,128)(2,1)S(1)}, bf16[1,128,2048]{1,2,0:T(8,128)(2,1)}, u32[]{:S(2)}) copy-start(bf16[1,128,2048]{1,2,0:T(8,128)(2,1)} %copy.107) | copy-start | bytes 1572868
  192.1 1.0 copy-start.5
  205.6 11.9 %copy-start.14 = (bf16[4096,128]{1,0:T(8,128)(2,1)S(1)}, bf16[4096,128]{1,0:T(8,128)(2,1)}, u32[]{:S(2)}) copy-start(bf16[4096,128]{1,0:T(8,128)(2,1)} %get-tuple-element.98) | copy-start | bytes 3145732
  205.6 14.4 %slice-start = ((s8[17301504]{0:T(1024)(128)(4,1)}), s8[4194304]{0:T(1024)(128)(4,1)S(1)}, s32[]{:S(2)}) async-start(s8[17301504]{0:T(1024)(128)(4,1)} %bitcast.158), calls=%async_computation.11 | async-start | bytes 8388608
  205.6 14.4 %slice-start.1 = ((s8[17301504]{0:T(1024)(128)(4,1)}), s8[4194304]{0:T(1024)(128)(4,1)S(1)}, s32[]{:S(2)}) async-start(s8[17301504]{0:T(1024)(128)(4,1)} %bitcast.158), calls=%async_computation.12 | async-start | bytes 8388608
  205.6 14.4 %slice-start.2 = ((s8[17301504]{0:T(1024)(128)(4,1)}), s8[4194304]{0:T(1024)(128)(4,1)S(1)}, s32[]{:S(2)}) async-start(s8[17301504]{0:T(1024)(128)(4,1)} %bitcast.158), calls=%async_computation.13 | async-start | bytes 8388608
  205.6 14.4 %slice-start.3 = ((s8[17301504]{0:T(1024)(128)(4,1)}), s8[4194304]{0:T(1024)(128)(4,1)S(1)}, s32[]{:S(2)}) async-start(s8[17301504]{0:T(1024)(128)(4,1)} %bitcast.158), calls=%async_computation.14 | async-start | bytes 8388608
  213.1 4.4 copy-start.3
  217.5 2.6 slice-start.4
  220.2 7.2 %copy-start.8 = (bf16[1,128,2048]{1,2,0:T(8,128)(2,1)S(1)}, bf16[1,128,2048]{1,2,0:T(8,128)(2,1)}, u32[]{:S(2)}) copy-start(bf16[1,128,2048]{1,2,0:T(8,128)(2,1)} %copy.107) | copy-start | bytes 1572868
  227.4 7.5 %slice-start.10 = ((bf16[4224,128]{0,1:T(8,128)(2,1)}), bf16[4096,128]{0,1:T(8,128)(2,1)S(1)}, s32[]{:S(2)}) async-start(bf16[4224,128]{0,1:T(8,128)(2,1)} %copy-done.5), calls=%async_computation.21 | async-start | bytes 2097152 | tf_op jit(solution)/shard_map/slice | solution.py:135
  233.8 1.0 copy-start.11
  234.8 1.7 copy-start.10
  236.5 106.4 %reduce-scatter.6.cloned.1.call-start = ((), (), s32[]{:S(2)}) async-start(), calls=%async_computation.8 | async-start | bytes 2359296 | tf_op jit(solution)/shard_map/reduce_scatter | solution.py:148
  242.9 1.0 copy-start.13
  250.5 1.7 copy-start.12
  252.2 179.7 %reduce-scatter.8.cloned.1.call-start = ((), (), s32[]{:S(2)}) async-start(), calls=%async_computation.9 | async-start | bytes 10485760 | tf_op jit(solution)/shard_map/reduce_scatter | solution.py:164
  354.3 0.8 copy-start.22
  354.3 77.5 %copy-start = (bf16[1,128,8192]{2,1,0:T(8,128)(2,1)S(1)}, bf16[1,128,8192]{2,1,0:T(8,128)(2,1)}, u32[]{:S(2)}) copy-start(bf16[1,128,8192]{2,1,0:T(8,128)(2,1)} %param.21) | copy-start | bytes 6291460
  354.4 165.8 %all-gather.9.cloned.1.call-start = ((), (), s32[]{:S(2)}) async-start(), calls=%async_computation.10 | async-start | bytes 10485760 | tf_op jit(solution)/shard_map/all_gather | solution.py:18
  431.9 2.8 copy-start.1
  434.7 2.9 copy-start.19
  442.7 14.4 %copy-start.16 = (bf16[512,256]{0,1:T(8,128)(2,1)S(1)}, bf16[512,256]{0,1:T(8,128)(2,1)}, u32[]{:S(2)}) copy-start(bf16[512,256]{0,1:T(8,128)(2,1)} %reduce-scatter.4.cloned.1.call-done) | copy-start | bytes 786436
  453.7 10.9 %all-to-all-start.1 = ((bf16[4,128,256]{1,2,0:T(8,128)(2,1)}), bf16[4,128,256]{1,2,0:T(8,128)(2,1)S(1)}, u32[]{:S(2)}, u32[]{:S(2)}) async-start(bf16[4,128,256]{1,2,0:T(8,128)(2,1)} %copy_bitcast_fusion), calls=%async_computation.3 | async-start | bytes 524288 | tf_op jit(solution)/shard_map/all_to_all | solution.py:156
  464.6 10.9 %all-to-all-start = ((bf16[4,128,256]{1,2,0:T(8,128)(2,1)}), bf16[4,128,256]{1,2,0:T(8,128)(2,1)S(1)}, u32[]{:S(2)}, u32[]{:S(2)}) async-start(bf16[4,128,256]{1,2,0:T(8,128)(2,1)} %copy_bitcast_fusion.1), calls=%async_computation.1 | async-start | bytes 524288 | tf_op jit(solution)/shard_map/all_to_all | solution.py:153
Sparse Core Ops, SparseCore 0:
  9.7 68.6 all-gather.4
  80.2 65.5 all-gather.6
  236.6 52.1 reduce-scatter.3
  291.0 51.8 reduce-scatter.5
  354.5 77.3 reduce-scatter.7
  437.7 82.4 all-gather.8
where the time goes:
time: 557 us; the launch traced here: 552 us
  waiting for transfers between devices  356 us (64%)
  matrix products  71.5 us (13%)
  other arithmetic  67.1 us (12%)
  local copies, waits for them, and re-layouts  35.1 us (6%)
  between operations  15 us (3%)
  starting transfers between devices  7.31 us (1%)
    reduce_scatter x1, waiting for transfers between devices, on_device(): lax.psum_scatter(lax.dot_general(stacked, weight_local, (((1, 2), (1, 2))...  76.7 us
    all_gather x1, waiting for transfers between devices, on_device(): lax.all_gather(prefix_values, ('sample', 'tensor'), axis=1, tiled=True)  67.3 us
    all_gather x1, waiting for transfers between devices, on_device(): lax.all_gather(prefix_keys, ('sample', 'tensor'), axis=1, tiled=True)  64.6 us
    reduce_scatter x1, waiting for transfers between devices, on_device(): lax.psum_scatter(pooled_value.astype(jnp.bfloat16), 'sample', scatter_dim...  54.1 us
    all_gather x1, waiting for transfers between devices, entering(): gathered = lax.all_gather(value.astype(jnp.bfloat16), axis)  43.6 us
    reduce_scatter x1, waiting for transfers between devices, on_device(): lax.psum_scatter(pooled_key.astype(jnp.bfloat16), 'sample', scatter_dimen...  36.3 us
    unnamed x81, local copies, waits for them, and re-layouts  22.6 us
    sub x2, other arithmetic, attend_group(): exponent = jnp.exp(scores - row_max)  20.9 us
  transfers between devices with their start and end apart: 8, of which 8 were waited for; matrix products, arithmetic and copies ran while one was open for 7% of the time, Pallas kernels for 0%

commit v1 on v0

v1 whole, which is shorter than its diff:
```python
import jax
import jax.numpy as jnp
from jax import lax
from jax.sharding import PartitionSpec as P

HEAD_SIZE = 128
PAGE = 128


MASKED_SCORE = -1e30
EPSILON = 1e-05


def visible_keys(seg_row, prompt_row, table, pooled_rows):
    tok_count = seg_row.shape[0]
    seg_hot = seg_row[:, None] == jnp.arange(prompt_row.shape[0], dtype=jnp.int32)[None, :]
    prompt_tok = jnp.sum(jnp.where(seg_hot, prompt_row[None, :], 0), axis=1)
    page_ids = jnp.arange(pooled_rows // PAGE, dtype=jnp.int32)
    member = jnp.any(table[:, :, None] == page_ids[None, None, :], axis=1)
    prompt_hot = prompt_tok[:, None] == jnp.arange(table.shape[0], dtype=jnp.int32)[None, :]
    member_tok = jnp.any(prompt_hot[:, :, None] & member[None, :, :], axis=1)
    prefix_seen = jnp.repeat(member_tok, PAGE, axis=1)
    position = jnp.arange(tok_count, dtype=jnp.int32)
    suffix_seen = (seg_row[:, None] == seg_row[None, :]) & (position[None, :] <= position[:, None])
    return jnp.concatenate([prefix_seen, suffix_seen], axis=1)


def attend_group(query_grp, grad_grp, key_rows, value_rows, visible):
    inv_root = query_grp.shape[-1] ** (-0.5)
    scores = (
        jnp.einsum("rgd,kd->rgk", query_grp, key_rows, preferred_element_type=jnp.float32)
        * inv_root
    )
    scores = jnp.where(visible[:, None, :], scores, MASKED_SCORE)
    row_max = jnp.max(scores, axis=2, keepdims=True)
    exponent = jnp.exp(scores - row_max)
    softmax_w = exponent / jnp.sum(exponent, axis=2, keepdims=True)
    weights_low = softmax_w.astype(jnp.bfloat16)
    attended = jnp.einsum(
        "rgk,kd->rgd", weights_low, value_rows, preferred_element_type=jnp.float32
    )
    delta_row = jnp.sum(grad_grp.astype(jnp.float32) * attended, axis=2, keepdims=True)
    weight_grad = jnp.einsum(
        "rgd,kd->rgk", grad_grp, value_rows, preferred_element_type=jnp.float32
    )
    score_grad = (softmax_w * (weight_grad - delta_row)).astype(jnp.bfloat16)
    query_out = (
        jnp.einsum("rgk,kd->rgd", score_grad, key_rows, preferred_element_type=jnp.float32)
        * inv_root
    )
    key_result = (
        jnp.einsum("rgk,rgd->kd", score_grad, query_grp, preferred_element_type=jnp.float32)
        * inv_root
    )
    value_out = jnp.einsum("rgk,rgd->kd", weights_low, grad_grp, preferred_element_type=jnp.float32)
    return (query_out, key_result, value_out)


def make_body(n_sec, n_smp, n_ten):
    def on_device(
        queries,
        suffix_keys,
        suffix_values,
        output_grad,
        prefix_keys,
        prefix_values,
        kv_weight,
        prefix_states,
        norm_gain,
        segment_ids,
        segment_prompt,
        block_table,
    ):
        head_width = suffix_keys.shape[2]
        kv_local = head_width // HEAD_SIZE
        rows_local = prefix_keys.shape[1]
        pooled_rows = rows_local * n_smp * n_ten
        block_rows = rows_local * n_ten
        tok_count = queries.shape[1]
        group_size = queries.shape[2] // head_width
        visible = visible_keys(segment_ids[0], segment_prompt[0], block_table, pooled_rows)
        query_rows = queries[0].reshape(tok_count, kv_local, group_size, HEAD_SIZE)
        grad_rows = output_grad[0].reshape(tok_count, kv_local, group_size, HEAD_SIZE)
        own_keys = suffix_keys[0]
        own_values = suffix_values[0]
        pk = prefix_keys[0].reshape(rows_local, n_ten, kv_local, HEAD_SIZE)
        pv = prefix_values[0].reshape(rows_local, n_ten, kv_local, HEAD_SIZE)

        query_pieces, suffix_key_pieces, suffix_value_pieces, reduced_pieces = [], [], [], []
        for head_index in range(kv_local):
            low_col = head_index * HEAD_SIZE
            send = jnp.concatenate([pk[:, :, head_index], pv[:, :, head_index]], axis=-1)
            send = send.transpose(1, 0, 2)
            got = lax.all_to_all(send, "tensor", 0, 0, tiled=True)
            got = got.reshape(block_rows, 2 * HEAD_SIZE)
            pool = lax.all_gather(got, "sample", axis=0, tiled=True)
            key_rows = jnp.concatenate(
                [pool[:, :HEAD_SIZE], own_keys[:, low_col : low_col + HEAD_SIZE]], axis=0
            )
            value_rows = jnp.concatenate(
                [pool[:, HEAD_SIZE:], own_values[:, low_col : low_col + HEAD_SIZE]], axis=0
            )
            query_out, key_result, value_out = attend_group(
                query_rows[:, head_index], grad_rows[:, head_index], key_rows, value_rows, visible
            )
            query_pieces.append(query_out)
            suffix_key_pieces.append(key_result[pooled_rows:])
            suffix_value_pieces.append(value_out[pooled_rows:])
            pool_grad = jnp.concatenate(
                [key_result[:pooled_rows], value_out[:pooled_rows]], axis=1
            ).astype(jnp.bfloat16)
            reduced_pieces.append(
                lax.psum_scatter(pool_grad, "sample", scatter_dimension=0, tiled=True)
            )
        query_grad = jnp.stack(query_pieces, axis=1).reshape(tok_count, -1).astype(jnp.bfloat16)
        rollout_key_gradient = jnp.concatenate(suffix_key_pieces, axis=1).astype(jnp.bfloat16)
        suffix_value_grad = jnp.concatenate(suffix_value_pieces, axis=1).astype(jnp.bfloat16)

        reduced = jnp.concatenate(reduced_pieces, axis=1)
        home_send = reduced.reshape(n_ten, rows_local, kv_local * 2 * HEAD_SIZE)
        home = lax.all_to_all(home_send, "tensor", 0, 0, tiled=True)
        home = home.reshape(n_ten, rows_local, kv_local, 2, HEAD_SIZE).transpose(3, 1, 0, 2, 4)
        home = home.reshape(2, rows_local, n_ten * kv_local * HEAD_SIZE).astype(jnp.float32)
        key_home = home[0]
        value_home = home[1]

        grad_cols = reduced.reshape(block_rows, kv_local, 2, HEAD_SIZE).transpose(0, 2, 1, 3)
        grad_cols = grad_cols.reshape(block_rows, 2, kv_local * HEAD_SIZE)
        group_term = lax.dot_general(
            grad_cols, kv_weight[0], (((1, 2), (1, 2)), ((), ())), preferred_element_type=jnp.float32
        ).astype(jnp.bfloat16)
        width = group_term.shape[1]
        t_idx = lax.axis_index("tensor")
        core = t_idx % 2
        hi = t_idx // 2
        term4 = group_term.reshape(2, 2, rows_local, width)
        keep = lax.dynamic_index_in_dim(term4, core, 1, False)
        give = lax.dynamic_index_in_dim(term4, 1 - core, 1, False)
        core_pairs = [(i, i ^ 1) for i in range(n_ten)]
        got1 = lax.ppermute(give, "tensor", core_pairs)
        partial = keep.astype(jnp.float32) + got1.astype(jnp.float32)
        mine = lax.dynamic_index_in_dim(partial, hi, 0, False)
        other = lax.dynamic_index_in_dim(partial, 1 - hi, 0, False)
        chip_pairs = [(i, i ^ 2) for i in range(n_ten)]
        got2 = lax.ppermute(other.astype(jnp.bfloat16), "tensor", chip_pairs)
        normed_grad = mine + got2.astype(jnp.float32)

        states = prefix_states[0].astype(jnp.float32)
        gain_wide = norm_gain[0].astype(jnp.float32)[None, :]
        inv_rms = lax.rsqrt(jnp.mean(states * states, axis=1, keepdims=True) + EPSILON)
        gained = gain_wide * normed_grad
        layer_term = inv_rms * gained - states * inv_rms**3 * jnp.mean(
            states * gained, axis=1, keepdims=True
        )
        term_low = layer_term.astype(jnp.bfloat16)
        prefix_state_gradient = layer_term
        for shift in range(1, n_sec):
            pairs = [(l + shift, l) for l in range(n_sec - shift)]
            prefix_state_gradient = prefix_state_gradient + lax.ppermute(
                term_low, "section", pairs
            ).astype(jnp.float32)
        return (
            query_grad[None],
            rollout_key_gradient[None],
            suffix_value_grad[None],
            key_home[None],
            value_home[None],
            prefix_state_gradient[None],
        )

    return on_device


def solution(mesh):
    placed = (
        P("section", "sample", "tensor"),
        P("section", "sample", "tensor"),
        P("section", "sample", "tensor"),
        P("section", "sample", "tensor"),
        P("section", ("sample", "tensor"), None),
        P("section", ("sample", "tensor"), None),
        P("section", None, None, "tensor"),
        P("section", ("sample", "tensor"), None),
        P("section", None),
        P("sample", None),
        P("sample", None),
        P(),
    )
    body = make_body(mesh.shape["section"], mesh.shape["sample"], mesh.shape["tensor"])
    return jax.shard_map(
        body,
        mesh=mesh,
        in_specs=placed,
        out_specs=(
            P("section", "sample", "tensor"),
            P("section", "sample", "tensor"),
            P("section", "sample", "tensor"),
            P("section", ("sample", "tensor"), None),
            P("section", ("sample", "tensor"), None),
            P("section", ("sample", "tensor"), None),
        ),
        check_vma=False,
    )
```

time: 557 us -> 448 us (0.80)
  waiting for transfers between devices: 356 us -> 231 us
  matrix products: 71.5 us -> 57.7 us
  local copies, waits for them, and re-layouts: 35.1 us -> 48.1 us
  blocking collectives: 0 us -> 12 us
  starting transfers between devices: 7.31 us -> 14.5 us
    all_gather x3 -> x2, waiting for transfers between devices: 176 us -> 44.8 us  [on_device(): pool = lax.all_gather(got, 'sample', axis=0, tiled=True)]
    ppermute x0 -> x5, waiting for transfers between devices: none -> 119 us  [the longest x3 69.9 us: on_device(): lax.ppermute(term_low, 'section', pairs).astype(jnp.float32)]
    reduce_scatter x3 -> x2, waiting for transfers between devices: 167 us -> 57.2 us  [on_device(): lax.psum_scatter(pool_grad, 'sample', scatter_dimension=0, tiled=True)]
    all_to_all x0 -> x1, blocking collectives: none -> 12 us  [on_device(): got = lax.all_to_all(send, 'tensor', 0, 0, tiled=True)]
    add x3 -> x1, other arithmetic: 15.9 us -> 4.9 us  [on_device(): partial = keep.astype(jnp.float32) + got1.astype(jnp.float32)]
    dot_general x2, matrix products: 12.8 us -> 5.78 us  [attend_group(): jnp.einsum('rgk,rgd->kd', weights_low, grad_grp, preferred_element_type=j...]
    ppermute x0 -> x5, starting transfers between devices: none -> 6.72 us  [the longest x3 4 us: on_device(): lax.ppermute(term_low, 'section', pairs).astype(jnp.float32)]
    slice x7 -> x11, local copies, waits for them, and re-layouts: 1.89 us -> 8.48 us  [the longest x2 5.29 us: on_device(): pool[:, HEAD_SIZE:]]
  transfers between devices with their start and end apart: 8 -> 11, of which waited for: 8 -> 9; matrix products, arithmetic and copies ran while one was open for 7% -> 24% of each run, Pallas kernels for 0% -> 0%
where the time goes in v1:
time: 448 us; the launch traced here: 441 us
  waiting for transfers between devices  231 us (52%)
  other arithmetic  62.2 us (14%)
  matrix products  57.7 us (13%)
  local copies, waits for them, and re-layouts  48.1 us (11%)
  between operations  14.7 us (3%)
  starting transfers between devices  14.5 us (3%)
  blocking collectives  12 us (3%)
    ppermute x3, waiting for transfers between devices, on_device(): lax.ppermute(term_low, 'section', pairs).astype(jnp.float32)  69.9 us
    reduce_scatter x2, waiting for transfers between devices, on_device(): lax.psum_scatter(pool_grad, 'sample', scatter_dimension=0, tiled=True)  57.2 us
    all_gather x2, waiting for transfers between devices, on_device(): pool = lax.all_gather(got, 'sample', axis=0, tiled=True)  44.8 us
    ppermute x1, waiting for transfers between devices, on_device(): got2 = lax.ppermute(other.astype(jnp.bfloat16), 'tensor', chip_pairs)  41.7 us
    unnamed x100, local copies, waits for them, and re-layouts  23.1 us
    sub x2, other arithmetic, attend_group(): exponent = jnp.exp(scores - row_max)  21 us
    convert_element_type x2, other arithmetic, attend_group(): weights_low = softmax_w.astype(jnp.bfloat16)  15.1 us
    dot_general x2, matrix products, attend_group(): jnp.einsum('rgk,rgd->kd', score_grad, query_grp, preferred_element_type=j...  13 us
  transfers between devices with their start and end apart: 11, of which 9 were waited for; matrix products, arithmetic and copies ran while one was open for 24% of the time, Pallas kernels for 0%

profile of v1, /device:TPU:0, one launch (start us, length us, event | category | flops | bytes accessed | tf_op | source)
XLA Modules:
  0.0 440.6 jit_solution(18335856734817122372)
XLA Ops:
  7.2 1.2 reshape_squeeze.12
  8.4 1.1 reshape_squeeze.13
  10.4 12.0 %all_to_all.15 = bf16[4,128,256]{2,1,0:T(8,128)(2,1)} all-to-all(bf16[4,128,256]{2,1,0:T(8,128)(2,1)S(1)} %maximum_bitcast_fusion.12), channel_id=1, replica_groups=mesh['section'=4,'sample'=8,'tensor'=4] {'tensor'}, dimensions={0} | all-to-all | bytes 524288 | tf_op jit(solution)/shard_map/all_to_all | solution.py:94
  23.3 3.4 all-to-all-start.1
  27.3 0.9 copy.183
  29.6 1.4 fusion.65
  31.0 3.2 all-to-all-done.1
  34.9 39.9 %all-gather.3.cloned.1.call-done = bf16[4096,256]{1,0:T(8,128)(2,1)} async-done(((bf16[512,256]{1,0:T(8,128)(2,1)}), bf16[4096,256]{1,0:T(8,128)(2,1)}) %all-gather.3.cloned.1.call-update) | async-done | bytes 2097168 | tf_op jit(solution)/shard_map/all_gather | solution.py:96
  74.9 2.6 fusion.59
  77.5 1.0 copy-done.7
  78.5 2.4 fusion.34
  80.9 10.4 %fusion.68 = (f32[128,8]{0,1:T(8,128)S(1)}, f32[128,8,4224]{0,2,1:T(8,128)}) fusion(f32[4224,128,8]{1,0,2:T(8,128)S(1)} %fusion.34, pred[128,4224]{0,1:T(8,128)(4,1)S(1)} %pad_add_fusion), kind=kOutput, calls=%fused_computation.127 | output fusion | flops 17305728 | bytes 35147776 | tf_op jit(solution)/shard_map/sub | solution.py:36
  91.4 7.5 %fusion.13 = bf16[128,8,4224]{0,2,1:T(8,128)(2,1)S(1)} fusion(f32[128,8,4224]{0,2,1:T(8,128)} %get-tuple-element.53, f32[128,8]{0,1:T(8,128)S(1)} %get-tuple-element.52), kind=kLoop, calls=%fused_computation.23 | loop fusion | flops 8650752 | bytes 25956352 | tf_op jit(solution)/shard_map/convert_element_type | solution.py:38
  98.9 4.4 copy-done.5
  103.3 2.5 fusion.29
  106.1 6.2 %fusion.3 = bf16[128,8,4224]{0,2,1:T(8,128)(2,1)} fusion(f32[128,8]{0,1:T(8,128)S(1)} %fusion.29, f32[128,8,4224]{0,2,1:T(8,128)S(1)} %bitcast.189, f32[128,8]{0,1:T(8,128)S(1)} %get-tuple-element.52, bf16[128,128]{1,0:T(8,128)(2,1)} %get-tuple-element.44, bf16[4096,128]{1,0:T(8,128)(2,1)} %get-tuple-element.32, bf16[128,2,8,128]{0,3,2,1:T(8,128)(2,1)S(1)} %bitcast.199), kind=kOutput, calls=%fused_computation.6 | convolution fusion | flops 1126760448 | bytes 27303936 | tf_op jit(solution)/shard_map/rgd,kd->rgk/dot_general | solution.py:43
  112.2 6.5 %fusion.17 = bf16[4224,128]{0,1:T(8,128)(2,1)S(1)} fusion(bf16[128,8,4224]{0,2,1:T(8,128)(2,1)} %fusion.3, bf16[128,2,8,128]{0,3,2,1:T(8,128)(2,1)S(1)} %bitcast.194), kind=kOutput, calls=%fused_computation.34 | convolution fusion | flops 1108377600 | bytes 9994240 | tf_op jit(solution)/shard_map/rgk,rgd->kd/dot_general | solution.py:52
  118.9 2.9 fusion.19
  121.9 0.9 copy-done.14
  122.8 1.5 pad_maximum_fusion
  124.4 4.9 %all-gather.5.cloned.1.call-done = bf16[4096,256]{1,0:T(8,128)(2,1)} async-done(((bf16[512,256]{1,0:T(8,128)(2,1)}), bf16[4096,256]{1,0:T(8,128)(2,1)}) %all-gather.5.cloned.1.call-update) | async-done | bytes 2097168 | tf_op jit(solution)/shard_map/all_gather | solution.py:96
  129.3 2.6 fusion.60
  131.9 1.0 copy-done.9
  132.9 2.4 fusion.33
  135.3 10.6 %fusion.67 = (f32[128,8]{0,1:T(8,128)S(1)}, f32[128,8,4224]{0,2,1:T(8,128)}) fusion(f32[4224,128,8]{1,0,2:T(8,128)S(1)} %fusion.33, pred[128,4224]{0,1:T(8,128)(4,1)S(1)} %pad_add_fusion), kind=kOutput, calls=%fused_computation.126 | output fusion | flops 17305728 | bytes 35147776 | tf_op jit(solution)/shard_map/sub | solution.py:36
  146.0 7.6 %fusion.14 = bf16[128,8,4224]{0,2,1:T(8,128)(2,1)S(1)} fusion(f32[128,8,4224]{0,2,1:T(8,128)} %get-tuple-element.51, f32[128,8]{0,1:T(8,128)S(1)} %get-tuple-element.50), kind=kLoop, calls=%fused_computation.24 | loop fusion | flops 8650752 | bytes 25956352 | tf_op jit(solution)/shard_map/convert_element_type | solution.py:38
  153.6 4.4 copy-done.3
  158.0 2.5 fusion.30
  160.7 6.1 %fusion.2 = bf16[128,8,4224]{0,2,1:T(8,128)(2,1)} fusion(f32[128,8]{0,1:T(8,128)S(1)} %fusion.30, f32[128,8,4224]{0,2,1:T(8,128)S(1)} %bitcast.187, f32[128,8]{0,1:T(8,128)S(1)} %get-tuple-element.50, bf16[128,128]{1,0:T(8,128)(2,1)S(1)} %copy-done.28, bf16[4096,128]{1,0:T(8,128)(2,1)} %get-tuple-element.34, bf16[128,2,8,128]{0,3,2,1:T(8,128)(2,1)S(1)} %bitcast.201), kind=kOutput, calls=%fused_computation.3 | convolution fusion | flops 1126760448 | bytes 27303936 | tf_op jit(solution)/shard_map/rgd,kd->rgk/dot_general | solution.py:43
  166.8 6.5 %fusion.18 = bf16[4224,128]{0,1:T(8,128)(2,1)S(1)} fusion(bf16[128,8,4224]{0,2,1:T(8,128)(2,1)} %fusion.2, bf16[128,2,8,128]{0,3,2,1:T(8,128)(2,1)S(1)} %bitcast.196), kind=kOutput, calls=%fused_computation.35 | convolution fusion | flops 1108377600 | bytes 9994240 | tf_op jit(solution)/shard_map/rgk,rgd->kd/dot_general | solution.py:52
  173.3 1.0 copy-done.16
  174.4 2.9 fusion.20
  177.3 1.0 copy-done.15
  178.4 1.5 pad_maximum_fusion.1
  180.0 4.1 reduce-scatter.3.cloned.1.call-done
  184.1 1.0 constant_dynamic-update-slice_fusion.1
  185.1 53.1 %reduce-scatter.5.cloned.1.call-done = bf16[512,256]{0,1:T(8,128)(2,1)} async-done(((bf16[4096,256]{0,1:T(8,128)(2,1)}), bf16[512,256]{0,1:T(8,128)(2,1)}) %reduce-scatter.5.cloned.1.call-update) | async-done | bytes 262160 | tf_op jit(solution)/shard_map/reduce_scatter | solution.py:113
  238.2 1.0 constant_dynamic-update-slice_fusion
  240.0 10.3 %bitcast_convert_fusion = bf16[512,8192]{1,0:T(8,128)(2,1)} fusion(bf16[512,2,256]{2,0,1:T(8,128)(2,1)S(1)} %reshape.173, bf16[8192,2,256]{2,1,0:T(2,128)(2,1)} %bitcast.216), kind=kOutput, calls=%fused_computation.10 | convolution fusion | flops 4299161600 | bytes 17301504 | tf_op jit(solution)/shard_map/dot_general | solution.py:129
  250.3 4.6 %dynamic-slice_bitcast_fusion = bf16[2,128,8192]{2,1,0:T(8,128)(2,1)} fusion(bf16[2,2,128,8192]{3,2,1,0:T(8,128)(2,1)} %bitcast.190, s32[]{:T(128)S(6)} %select_n.41), kind=kLoop, calls=%fused_computation.46 | loop fusion | bytes 8388612 | tf_op jit(solution)/shard_map/jit(dynamic_index_in_dim)/squeeze | solution.py:138
  254.9 7.5 %collective-permute-done = bf16[2,128,8192]{2,1,0:T(8,128)(2,1)} collective-permute-done((bf16[2,128,8192]{2,1,0:T(8,128)(2,1)}, bf16[2,128,8192]{2,1,0:T(8,128)(2,1)}, u32[]{:S(2)}, u32[]{:S(2)}) %collective-permute-start) | collective-permute-done | bytes 4194336 | tf_op jit(solution)/shard_map/ppermute | solution.py:140
  262.4 4.9 %convert_add_fusion = f32[2,128,8192]{2,1,0:T(8,128)S(1)} fusion(bf16[2,128,8192]{2,1,0:T(8,128)(2,1)} %collective-permute-done, bf16[2,2,128,8192]{3,2,1,0:T(8,128)(2,1)} %bitcast.191, s32[]{:T(128)S(6)} %select_n.40), kind=kLoop, calls=%fused_computation.21 | loop fusion | flops 6291456 | bytes 16777220 | tf_op jit(solution)/shard_map/add | solution.py:141
  267.3 3.3 copy-done
  270.6 1.6 fusion.26
  272.2 2.7 collective-permute-start.1
  275.0 5.0 %fusion.32 = bf16[128,1,8,128]{0,3,2,1:T(8,128)(2,1)S(1)} fusion(bf16[128,8,4224]{0,2,1:T(8,128)(2,1)} %fusion.3, bf16[128,128]{1,0:T(8,128)(2,1)S(1)} %copy-done.25, bf16[4096,128]{1,0:T(8,128)(2,1)S(1)} %copy-done.8), kind=kOutput, calls=%fused_computation.60 | convolution fusion | flops 1109721088 | bytes 9994240 | tf_op jit(solution)/shard_map/rgk,kd->rgd/dot_general | solution.py:48
  280.0 41.7 %collective-permute-done.1 = bf16[128,8192]{1,0:T(8,128)(2,1)} collective-permute-done((bf16[128,8192]{1,0:T(8,128)(2,1)}, bf16[128,8192]{1,0:T(8,128)(2,1)}, u32[]{:S(2)}, u32[]{:S(2)}) %collective-permute-start.1) | collective-permute-done | bytes 2097184 | tf_op jit(solution)/shard_map/ppermute | solution.py:145
  321.7 3.0 fusion.21
  324.8 4.7 %fusion.58 = bf16[128,8192]{1,0:T(8,128)(2,1)} fusion(f32[128]{0:T(128)S(1)} %broadcast_multiply_fusion, f32[128]{0:T(128)S(1)} %get-tuple-element.49, bf16[1,128,8192]{2,1,0:T(8,128)(2,1)S(1)} %copy-done.2, bf16[128,8192]{1,0:T(8,128)(2,1)} %collective-permute-done.1, f32[2,128,8192]{2,1,0:T(8,128)S(1)} %copy-done.1, s32[]{:T(128)S(6)} %select_n.43, ...), kind=kLoop, calls=%fused_computation.117 | loop fusion | flops 9437184 | bytes 10520068 | tf_op jit(solution)/shard_map/convert_element_type | solution.py:155
  329.5 1.4 collective-permute-start.4
  331.0 1.3 collective-permute-start.3
  332.3 1.3 collective-permute-start.2
  333.6 1.4 fusion.31
  335.1 0.8 slice_bitcast_fusion.9
  335.9 0.8 slice_bitcast_fusion.7
  336.6 0.8 slice_bitcast_fusion.8
  337.4 0.9 copy_bitcast_fusion
  338.3 4.2 all-to-all-start.2
  342.5 1.0 copy.153
  345.7 7.0 %all-to-all-done.2 = bf16[4,128,512]{1,2,0:T(8,128)(2,1)S(1)} async-done(((bf16[4,128,512]{1,2,0:T(8,128)(2,1)}), bf16[4,128,512]{1,2,0:T(8,128)(2,1)S(1)}, u32[]{:S(2)}, u32[]{:S(2)}) %all-to-all-start.2) | async-done | bytes 524320 | tf_op jit(solution)/shard_map/all_to_all | solution.py:121
  352.9 1.0 copy.179
  353.9 1.0 copy.178
  354.9 69.9 %collective-permute-done.4 = bf16[128,8192]{1,0:T(8,128)(2,1)} collective-permute-done((bf16[128,8192]{1,0:T(8,128)(2,1)}, bf16[128,8192]{1,0:T(8,128)(2,1)}, u32[]{:S(2)}, u32[]{:S(2)}) %collective-permute-start.4) | collective-permute-done | bytes 2097184 | tf_op jit(solution)/shard_map/ppermute | solution.py:159
  424.9 9.0 %add_bitcast_fusion = f32[1,128,8192]{2,1,0:T(8,128)} fusion(bf16[128,8192]{1,0:T(8,128)(2,1)} %collective-permute-done.4, bf16[128,8192]{1,0:T(8,128)(2,1)} %collective-permute-done.3, bf16[128,8192]{1,0:T(8,128)(2,1)} %collective-permute-done.2, f32[128]{0:T(128)S(1)} %broadcast_multiply_fusion, f32[128]{0:T(128)S(1)} %get-tuple-element.49, ...), kind=kLoop, calls=%fused_computation.44 | loop fusion | flops 14680064 | bytes 18908676 | tf_op jit(solution)/shard_map/broadcast_in_dim | solution.py:168
  (133 shorter events, 8.6 us)
Async XLA Ops:
  7.2 19.6 %copy-start.20 = (bf16[1,128,2048]{2,1,0:T(8,128)(2,1)S(1)}, bf16[1,128,2048]{2,1,0:T(8,128)(2,1)}, u32[]{:S(2)}) copy-start(bf16[1,128,2048]{2,1,0:T(8,128)(2,1)} %param.12) | copy-start | bytes 1572868
  7.2 19.8 %copy-start.21 = (bf16[1,128,2048]{2,1,0:T(8,128)(2,1)S(1)}, bf16[1,128,2048]{2,1,0:T(8,128)(2,1)}, u32[]{:S(2)}) copy-start(bf16[1,128,2048]{2,1,0:T(8,128)(2,1)} %param.15) | copy-start | bytes 1572868
  7.2 67.7 %all-gather.3.cloned.1.call-start = ((), (), s32[]{:S(2)}) async-start(), calls=%async_computation.5 | async-start | bytes 2359296 | tf_op jit(solution)/shard_map/all_gather | solution.py:96
  10.3 18.1 %copy-start.30 = (s32[1,128]{1,0:T(1,128)S(1)}, s32[1,128]{1,0:T(1,128)}, u32[]{:S(2)}) copy-start(s32[1,128]{1,0:T(1,128)} %param.21) | copy-start | bytes 1540
  10.3 18.1 %copy-start.32 = (s32[1,2]{1,0:T(1,128)S(1)}, s32[1,2]{1,0:T(1,128)}, u32[]{:S(2)}) copy-start(s32[1,2]{1,0:T(1,128)} %param.22) | copy-start | bytes 28
  10.3 18.2 %copy-start.31 = (s32[3,16]{1,0:T(4,128)S(1)}, s32[3,16]{1,0:T(4,128)}, u32[]{:S(2)}) copy-start(s32[3,16]{1,0:T(4,128)} %param.23) | copy-start | bytes 580
  10.3 18.4 %copy-start.26 = (bf16[1,128,256]{2,1,0:T(8,128)(2,1)S(1)}, bf16[1,128,256]{2,1,0:T(8,128)(2,1)}, u32[]{:S(2)}) copy-start(bf16[1,128,256]{2,1,0:T(8,128)(2,1)} %param.13) | copy-start | bytes 196612
  23.3 10.9 %all-to-all-start.1 = ((bf16[4,128,256]{2,1,0:T(8,128)(2,1)}), bf16[4,128,256]{2,1,0:T(8,128)(2,1)S(1)}, u32[]{:S(2)}, u32[]{:S(2)}) async-start(bf16[4,128,256]{2,1,0:T(8,128)(2,1)} %maximum_bitcast_fusion.13), calls=%async_computation.1 | async-start | bytes 524288 | tf_op jit(solution)/shard_map/all_to_all | solution.py:94
  26.7 102.6 %all-gather.5.cloned.1.call-start = ((), (), s32[]{:S(2)}) async-start(), calls=%async_computation.6 | async-start | bytes 2359296 | tf_op jit(solution)/shard_map/all_gather | solution.py:96
  34.1 0.7 copy-start.17
  34.9 43.7 %copy-start.24 = (bf16[128,128]{1,0:T(8,128)(2,1)S(1)}, bf16[128,128]{1,0:T(8,128)(2,1)}, u32[]{:S(2)}) copy-start(bf16[128,128]{1,0:T(8,128)(2,1)} %get-tuple-element.46) | copy-start | bytes 98308
  34.9 149.2 %reduce-scatter.3.cloned.1.call-start = ((), (), s32[]{:S(2)}) async-start(), calls=%async_computation.7 | async-start | bytes 2359296 | tf_op jit(solution)/shard_map/reduce_scatter | solution.py:113
  77.5 1.0 copy-start.7
  91.3 12.0 %copy-start.19 = (bf16[4096,128]{1,0:T(8,128)(2,1)S(1)}, bf16[4096,128]{1,0:T(8,128)(2,1)}, u32[]{:S(2)}) copy-start(bf16[4096,128]{1,0:T(8,128)(2,1)} %get-tuple-element.32) | copy-start | bytes 3145732
  91.3 12.0 %copy-start.22 = (bf16[128,1,8,128]{3,0,2,1:T(8,128)(2,1)S(1)}, bf16[128,1,8,128]{3,0,2,1:T(8,128)(2,1)}, u32[]{:S(2)}) copy-start(bf16[128,1,8,128]{3,0,2,1:T(8,128)(2,1)} %copy.183) | copy-start | bytes 786436
  91.3 12.0 %copy-start.29 = (bf16[128,128]{1,0:T(8,128)(2,1)S(1)}, bf16[128,128]{1,0:T(8,128)(2,1)}, u32[]{:S(2)}) copy-start(bf16[128,128]{1,0:T(8,128)(2,1)} %get-tuple-element.44) | copy-start | bytes 98308
  91.3 14.5 %slice-start.5 = ((s8[17301504]{0:T(1024)(128)(4,1)}), s8[4194304]{0:T(1024)(128)(4,1)S(1)}, s32[]{:S(2)}) async-start(s8[17301504]{0:T(1024)(128)(4,1)} %bitcast.188), calls=%async_computation.14 | async-start | bytes 8388608
  91.3 14.5 %slice-start.6 = ((s8[17301504]{0:T(1024)(128)(4,1)}), s8[4194304]{0:T(1024)(128)(4,1)S(1)}, s32[]{:S(2)}) async-start(s8[17301504]{0:T(1024)(128)(4,1)} %bitcast.188), calls=%async_computation.15 | async-start | bytes 8388608
  91.3 14.5 %slice-start.7 = ((s8[17301504]{0:T(1024)(128)(4,1)}), s8[4194304]{0:T(1024)(128)(4,1)S(1)}, s32[]{:S(2)}) async-start(s8[17301504]{0:T(1024)(128)(4,1)} %bitcast.188), calls=%async_computation.16 | async-start | bytes 8388608
  91.4 14.5 %slice-start.8 = ((s8[17301504]{0:T(1024)(128)(4,1)}), s8[4194304]{0:T(1024)(128)(4,1)S(1)}, s32[]{:S(2)}) async-start(s8[17301504]{0:T(1024)(128)(4,1)} %bitcast.188), calls=%async_computation.17 | async-start | bytes 8388608
  98.9 4.4 copy-start.5
  103.3 2.7 slice-start.9
  112.2 6.7 %copy-start.6 = (bf16[128,8,4224]{0,2,1:T(8,128)(2,1)S(1)}, bf16[128,8,4224]{0,2,1:T(8,128)(2,1)}, u32[]{:S(2)}) copy-start(bf16[128,8,4224]{0,2,1:T(8,128)(2,1)} %copy-done.5) | copy-start | bytes 25952260
  118.7 3.0 copy-start.13
  121.8 1.0 copy-start.14
  124.3 8.6 %copy-start.23 = (bf16[128,128]{1,0:T(8,128)(2,1)S(1)}, bf16[128,128]{1,0:T(8,128)(2,1)}, u32[]{:S(2)}) copy-start(bf16[128,128]{1,0:T(8,128)(2,1)} %get-tuple-element.47) | copy-start | bytes 98308
  124.3 113.9 %reduce-scatter.5.cloned.1.call-start = ((), (), s32[]{:S(2)}) async-start(), calls=%async_computation.8 | async-start | bytes 2359296 | tf_op jit(solution)/shard_map/reduce_scatter | solution.py:113
  131.9 1.0 copy-start.9
  146.0 12.0 %copy-start.18 = (bf16[4096,128]{1,0:T(8,128)(2,1)S(1)}, bf16[4096,128]{1,0:T(8,128)(2,1)}, u32[]{:S(2)}) copy-start(bf16[4096,128]{1,0:T(8,128)(2,1)} %get-tuple-element.34) | copy-start | bytes 3145732
  146.0 12.0 %copy-start.28 = (bf16[128,128]{1,0:T(8,128)(2,1)S(1)}, bf16[128,128]{1,0:T(8,128)(2,1)}, u32[]{:S(2)}) copy-start(bf16[128,128]{1,0:T(8,128)(2,1)} %get-tuple-element.45) | copy-start | bytes 98308
  146.0 14.5 %slice-start = ((s8[17301504]{0:T(1024)(128)(4,1)}), s8[4194304]{0:T(1024)(128)(4,1)S(1)}, s32[]{:S(2)}) async-start(s8[17301504]{0:T(1024)(128)(4,1)} %bitcast.186), calls=%async_computation.9 | async-start | bytes 8388608
  146.0 14.5 %slice-start.1 = ((s8[17301504]{0:T(1024)(128)(4,1)}), s8[4194304]{0:T(1024)(128)(4,1)S(1)}, s32[]{:S(2)}) async-start(s8[17301504]{0:T(1024)(128)(4,1)} %bitcast.186), calls=%async_computation.10 | async-start | bytes 8388608
  146.0 14.5 %slice-start.2 = ((s8[17301504]{0:T(1024)(128)(4,1)}), s8[4194304]{0:T(1024)(128)(4,1)S(1)}, s32[]{:S(2)}) async-start(s8[17301504]{0:T(1024)(128)(4,1)} %bitcast.186), calls=%async_computation.11 | async-start | bytes 8388608
  146.0 14.5 %slice-start.3 = ((s8[17301504]{0:T(1024)(128)(4,1)}), s8[4194304]{0:T(1024)(128)(4,1)S(1)}, s32[]{:S(2)}) async-start(s8[17301504]{0:T(1024)(128)(4,1)} %bitcast.186), calls=%async_computation.12 | async-start | bytes 8388608
  153.6 4.4 copy-start.3
  157.9 2.7 slice-start.4
  166.8 7.6 %copy-start.4 = (bf16[128,8,4224]{0,2,1:T(8,128)(2,1)S(1)}, bf16[128,8,4224]{0,2,1:T(8,128)(2,1)}, u32[]{:S(2)}) copy-start(bf16[128,8,4224]{0,2,1:T(8,128)(2,1)} %copy-done.3) | copy-start | bytes 25952260
  173.3 1.0 copy-start.16
  177.3 1.0 copy-start.15
  239.2 11.1 %copy-start.11 = (bf16[512,512]{0,1:T(8,128)(2,1)}, bf16[512,512]{0,1:T(8,128)(2,1)S(1)}, u32[]{:S(2)}) copy-start(bf16[512,512]{0,1:T(8,128)(2,1)S(1)} %constant_dynamic-update-slice_fusion) | copy-start | bytes 1572868
  254.9 7.5 %collective-permute-start = (bf16[2,128,8192]{2,1,0:T(8,128)(2,1)}, bf16[2,128,8192]{2,1,0:T(8,128)(2,1)}, u32[]{:S(2)}, u32[]{:S(2)}) collective-permute-start(bf16[2,128,8192]{2,1,0:T(8,128)(2,1)} %dynamic-slice_bitcast_fusion), channel_id=1, source_target_pairs={{0,1},{1,0},{2,3},{3,2},{4,5},{5,4},{6,7},{7,6},{8,9},{9,8},{10,11... | collective-permute-start | bytes 12582920 | tf_op jit(solution)/shard_map/ppermute | solution.py:140
  267.3 3.3 copy-start
  270.6 4.3 copy-start.27
  270.6 4.3 copy-start.8
  270.6 4.4 copy-start.25
  272.2 49.5 %collective-permute-start.1 = (bf16[128,8192]{1,0:T(8,128)(2,1)}, bf16[128,8192]{1,0:T(8,128)(2,1)}, u32[]{:S(2)}, u32[]{:S(2)}) collective-permute-start(bf16[128,8192]{1,0:T(8,128)(2,1)} %fusion.26), channel_id=1, source_target_pairs={{0,2},{1,3},{2,0},{3,1},{4,6},{5,7},{6,4},{7,5},{8,10},{9,11},{10,... | collective-permute-start | bytes 6291464 | tf_op jit(solution)/shard_map/ppermute | solution.py:145
  275.0 46.7 %copy-start.1 = (f32[2,128,8192]{2,1,0:T(8,128)S(1)}, f32[2,128,8192]{2,1,0:T(8,128)}, u32[]{:S(2)}) copy-start(f32[2,128,8192]{2,1,0:T(8,128)} %copy-done) | copy-start | bytes 25165828
  275.0 46.7 %copy-start.2 = (bf16[1,128,8192]{2,1,0:T(8,128)(2,1)S(1)}, bf16[1,128,8192]{2,1,0:T(8,128)(2,1)}, u32[]{:S(2)}) copy-start(bf16[1,128,8192]{2,1,0:T(8,128)(2,1)} %param.19) | copy-start | bytes 6291460
  321.7 11.8 %slice-start.10 = ((s8[8650752]{0:T(1024)(128)(4,1)}), s8[4194304]{0:T(1024)(128)(4,1)S(1)}, s32[]{:S(2)}) async-start(s8[8650752]{0:T(1024)(128)(4,1)} %bitcast.218), calls=%async_computation.19 | async-start | bytes 8388608
  321.7 11.8 %slice-start.11 = ((s8[8650752]{0:T(1024)(128)(4,1)}), s8[4194304]{0:T(1024)(128)(4,1)S(1)}, s32[]{:S(2)}) async-start(s8[8650752]{0:T(1024)(128)(4,1)} %bitcast.218), calls=%async_computation.20 | async-start | bytes 8388608
  324.8 8.8 %copy-start.10 = (bf16[4096,128]{1,0:T(8,128)(2,1)S(1)}, bf16[4096,128]{1,0:T(8,128)(2,1)}, u32[]{:S(2)}) copy-start(bf16[4096,128]{1,0:T(8,128)(2,1)} %copy-done.9) | copy-start | bytes 3145732
  324.8 8.8 %slice-start.12 = ((s8[8650752]{0:T(1024)(128)(4,1)}), s8[262144]{0:T(1024)(128)(4,1)S(1)}, s32[]{:S(2)}) async-start(s8[8650752]{0:T(1024)(128)(4,1)} %bitcast.218), calls=%async_computation.21 | async-start | bytes 524288
  329.5 7.8 %copy-start.12 = (bf16[512,512]{0,1:T(8,128)(2,1)S(1)}, bf16[512,512]{0,1:T(8,128)(2,1)}, u32[]{:S(2)}) copy-start(bf16[512,512]{0,1:T(8,128)(2,1)} %copy-done.11) | copy-start | bytes 1572868
  329.5 95.3 %collective-permute-start.4 = (bf16[128,8192]{1,0:T(8,128)(2,1)}, bf16[128,8192]{1,0:T(8,128)(2,1)}, u32[]{:S(2)}, u32[]{:S(2)}) collective-permute-start(bf16[128,8192]{1,0:T(8,128)(2,1)} %fusion.58), channel_id=1, source_target_pairs={{96,0},{97,1},{98,2},{99,3},{100,4},{101,5},{102,6},{103,7},{104,8... | collective-permute-start | bytes 6291464 | tf_op jit(solution)/shard_map/ppermute | solution.py:159
  331.0 93.9 %collective-permute-start.3 = (bf16[128,8192]{1,0:T(8,128)(2,1)}, bf16[128,8192]{1,0:T(8,128)(2,1)}, u32[]{:S(2)}, u32[]{:S(2)}) collective-permute-start(bf16[128,8192]{1,0:T(8,128)(2,1)} %fusion.58), channel_id=1, source_target_pairs={{64,0},{96,32},{65,1},{97,33},{66,2},{98,34},{67,3},{99,35},{68,4}... | collective-permute-start | bytes 6291464 | tf_op jit(solution)/shard_map/ppermute | solution.py:159
  332.3 92.6 %collective-permute-start.2 = (bf16[128,8192]{1,0:T(8,128)(2,1)}, bf16[128,8192]{1,0:T(8,128)(2,1)}, u32[]{:S(2)}, u32[]{:S(2)}) collective-permute-start(bf16[128,8192]{1,0:T(8,128)(2,1)} %fusion.58), channel_id=1, source_target_pairs={{32,0},{64,32},{96,64},{33,1},{65,33},{97,65},{34,2},{66,34},{98,6... | collective-permute-start | bytes 6291464 | tf_op jit(solution)/shard_map/ppermute | solution.py:159
  338.3 14.5 %all-to-all-start.2 = ((bf16[4,128,512]{1,2,0:T(8,128)(2,1)}), bf16[4,128,512]{1,2,0:T(8,128)(2,1)S(1)}, u32[]{:S(2)}, u32[]{:S(2)}) async-start(bf16[4,128,512]{1,2,0:T(8,128)(2,1)} %copy_bitcast_fusion), calls=%async_computation.4 | async-start | bytes 1048576 | tf_op jit(solution)/shard_map/all_to_all | solution.py:121
Sparse Core Ops, SparseCore 0:
  22.6 52.2 all-gather.2
  77.1 52.1 all-gather.4
  132.3 51.7 reduce-scatter.2
  186.4 51.8 reduce-scatter.4

commit v2 on v1

--- a/solution.py
+++ b/solution.py
@@ -93,7 +93,8 @@
             send = send.transpose(1, 0, 2)
             got = lax.all_to_all(send, "tensor", 0, 0, tiled=True)
             got = got.reshape(block_rows, 2 * HEAD_SIZE)
-            pool = lax.all_gather(got, "sample", axis=0, tiled=True)
+            spread = jnp.broadcast_to(got[None], (n_smp,) + got.shape)
+            pool = lax.all_to_all(spread, "sample", 0, 0, tiled=True).reshape(pooled_rows, -1)
             key_rows = jnp.concatenate(
                 [pool[:, :HEAD_SIZE], own_keys[:, low_col : low_col + HEAD_SIZE]], axis=0
             )
@@ -109,14 +110,14 @@
             pool_grad = jnp.concatenate(
                 [key_result[:pooled_rows], value_out[:pooled_rows]], axis=1
             ).astype(jnp.bfloat16)
-            reduced_pieces.append(
-                lax.psum_scatter(pool_grad, "sample", scatter_dimension=0, tiled=True)
-            )
+            pool_grad = pool_grad.reshape(n_smp, block_rows, 2 * HEAD_SIZE)
+            parts = lax.all_to_all(pool_grad, "sample", 0, 0, tiled=False)
+            reduced_pieces.append(jnp.sum(parts.astype(jnp.float32), axis=0))
         query_grad = jnp.stack(query_pieces, axis=1).reshape(tok_count, -1).astype(jnp.bfloat16)
         rollout_key_gradient = jnp.concatenate(suffix_key_pieces, axis=1).astype(jnp.bfloat16)
         suffix_value_grad = jnp.concatenate(suffix_value_pieces, axis=1).astype(jnp.bfloat16)
 
-        reduced = jnp.concatenate(reduced_pieces, axis=1)
+        reduced = jnp.concatenate(reduced_pieces, axis=1).astype(jnp.bfloat16)
         home_send = reduced.reshape(n_ten, rows_local, kv_local * 2 * HEAD_SIZE)
         home = lax.all_to_all(home_send, "tensor", 0, 0, tiled=True)
         home = home.reshape(n_ten, rows_local, kv_local, 2, HEAD_SIZE).transpose(3, 1, 0, 2, 4)
@@ -153,12 +154,11 @@
             states * gained, axis=1, keepdims=True
         )
         term_low = layer_term.astype(jnp.bfloat16)
-        prefix_state_gradient = layer_term
-        for shift in range(1, n_sec):
-            pairs = [(l + shift, l) for l in range(n_sec - shift)]
-            prefix_state_gradient = prefix_state_gradient + lax.ppermute(
-                term_low, "section", pairs
-            ).astype(jnp.float32)
+        terms = lax.all_gather(term_low, "section")
+        above = jnp.arange(n_sec) > lax.axis_index("section")
+        prefix_state_gradient = layer_term + jnp.sum(
+            jnp.where(above[:, None, None], terms.astype(jnp.float32), 0.0), axis=0
+        )
         return (
             query_grad[None],
             rollout_key_gradient[None],

time: 448 us -> 430 us (0.960)
  waiting for transfers between devices: 231 us -> 189 us
  starting transfers between devices: 14.5 us -> 34.1 us
  blocking collectives: 12 us -> 0 us
  other arithmetic: 62.2 us -> 70.4 us
  matrix products: 57.7 us -> 63.9 us
    ppermute x3 -> x0, waiting for transfers between devices: 69.9 us -> none  [on_device(): lax.ppermute(term_low, 'section', pairs).astype(jnp.float32)]
    all_to_all x0 -> x4, waiting for transfers between devices: none -> 65.4 us  [the longest x2 42.6 us: on_device(): lax.all_to_all(spread, 'sample', 0, 0, tiled=True).reshape(pooled_rows, -1)]
    reduce_scatter x2 -> x0, waiting for transfers between devices: 57.2 us -> none  [on_device(): lax.psum_scatter(pool_grad, 'sample', scatter_dimension=0, tiled=True)]
    all_to_all x0 -> x4, starting transfers between devices: none -> 20 us  [the longest x2 10.2 us: on_device(): parts = lax.all_to_all(pool_grad, 'sample', 0, 0, tiled=False)]
    all_to_all x1 -> x0, blocking collectives: 12 us -> none  [on_device(): got = lax.all_to_all(send, 'tensor', 0, 0, tiled=True)]
    all_to_all x1 -> x2, waiting for transfers between devices: 3.16 us -> 14.1 us  [on_device(): got = lax.all_to_all(send, 'tensor', 0, 0, tiled=True)]
    reduce_sum x0 -> x3, other arithmetic: none -> 8.01 us  [the longest x1 5.64 us: on_device(): jnp.sum(jnp.where(above[:, None, None], terms.astype(jnp.float32), 0.0),...]
    ppermute x1, waiting for transfers between devices: 41.7 us -> 47.8 us  [on_device(): got2 = lax.ppermute(other.astype(jnp.bfloat16), 'tensor', chip_pairs)]
  transfers between devices with their start and end apart: 11 -> 10, of which waited for: 9 -> 9; matrix products, arithmetic and copies ran while one was open for 24% -> 18% of each run, Pallas kernels for 0% -> 0%
where the time goes in v2:
time: 430 us; the launch traced here: 422 us
  waiting for transfers between devices  189 us (44%)
  other arithmetic  70.4 us (16%)
  matrix products  63.9 us (15%)
  local copies, waits for them, and re-layouts  49.7 us (12%)
  starting transfers between devices  34.1 us (8%)
  between operations  15.2 us (4%)
    ppermute x1, waiting for transfers between devices, on_device(): got2 = lax.ppermute(other.astype(jnp.bfloat16), 'tensor', chip_pairs)  47.8 us
    all_gather x1, waiting for transfers between devices, on_device(): terms = lax.all_gather(term_low, 'section')  46.6 us
    all_to_all x2, waiting for transfers between devices, on_device(): lax.all_to_all(spread, 'sample', 0, 0, tiled=True).reshape(pooled_rows, -1)  42.6 us
    unnamed x99, local copies, waits for them, and re-layouts  26.3 us
    all_to_all x2, waiting for transfers between devices, on_device(): parts = lax.all_to_all(pool_grad, 'sample', 0, 0, tiled=False)  22.8 us
    sub x2, other arithmetic, attend_group(): exponent = jnp.exp(scores - row_max)  20.4 us
    convert_element_type x2, other arithmetic, attend_group(): weights_low = softmax_w.astype(jnp.bfloat16)  14.7 us
    all_to_all x2, waiting for transfers between devices, on_device(): got = lax.all_to_all(send, 'tensor', 0, 0, tiled=True)  14.1 us
  transfers between devices with their start and end apart: 10, of which 9 were waited for; matrix products, arithmetic and copies ran while one was open for 18% of the time, Pallas kernels for 0%

profile of v2, /device:TPU:0, one launch (start us, length us, event | category | flops | bytes accessed | tf_op | source)
XLA Modules:
  0.0 421.9 jit_solution(18200077883700860931)
XLA Ops:
  7.2 1.1 copy.88
  8.3 1.1 copy.89
  10.2 4.6 %all-to-all-start.2 = ((bf16[4,128,256]{1,2,0:T(8,128)(2,1)}), bf16[4,128,256]{1,2,0:T(8,128)(2,1)S(1)}, u32[]{:S(2)}, u32[]{:S(2)}) async-start(bf16[4,128,256]{1,2,0:T(8,128)(2,1)} %maximum_bitcast_fusion.14), calls=%async_computation.2 | async-start | bytes 524288 | tf_op jit(solution)/shard_map/all_to_all | solution.py:94
  15.5 6.8 %all-to-all-done.2 = bf16[4,128,256]{1,2,0:T(8,128)(2,1)S(1)} async-done(((bf16[4,128,256]{1,2,0:T(8,128)(2,1)}), bf16[4,128,256]{1,2,0:T(8,128)(2,1)S(1)}, u32[]{:S(2)}, u32[]{:S(2)}) %all-to-all-start.2) | async-done | bytes 262176 | tf_op jit(solution)/shard_map/all_to_all | solution.py:94
  22.3 3.4 all-to-all-start
  25.9 7.3 %all-to-all-done = bf16[4,128,256]{1,2,0:T(8,128)(2,1)S(1)} async-done(((bf16[4,128,256]{1,2,0:T(8,128)(2,1)}), bf16[4,128,256]{1,2,0:T(8,128)(2,1)S(1)}, u32[]{:S(2)}, u32[]{:S(2)}) %all-to-all-start) | async-done | bytes 262176 | tf_op jit(solution)/shard_map/all_to_all | solution.py:94
  33.2 1.5 broadcast_in_dim.95
  34.6 5.4 %all-to-all-start.3 = ((bf16[8,512,256]{2,1,0:T(8,128)(2,1)}), bf16[8,512,256]{2,1,0:T(8,128)(2,1)S(1)}, u32[]{:S(2)}, u32[]{:S(2)}) async-start(bf16[8,512,256]{2,1,0:T(8,128)(2,1)} %broadcast_in_dim.95), calls=%async_computation.3 | async-start | bytes 4194304 | tf_op jit(solution)/shard_map/all_to_all | solution.py:97
  40.1 1.3 copy.95
  43.2 23.5 %all-to-all-done.3 = bf16[8,512,256]{2,1,0:T(8,128)(2,1)S(1)} async-done(((bf16[8,512,256]{2,1,0:T(8,128)(2,1)}), bf16[8,512,256]{2,1,0:T(8,128)(2,1)S(1)}, u32[]{:S(2)}, u32[]{:S(2)}) %all-to-all-start.3) | async-done | bytes 2097184 | tf_op jit(solution)/shard_map/all_to_all | solution.py:97
  66.7 1.6 broadcast_in_dim.92
  68.3 4.3 %all-to-all-start.1 = ((bf16[8,512,256]{2,1,0:T(8,128)(2,1)}), bf16[8,512,256]{2,1,0:T(8,128)(2,1)}, u32[]{:S(2)}, u32[]{:S(2)}) async-start(bf16[8,512,256]{2,1,0:T(8,128)(2,1)} %broadcast_in_dim.92), calls=%async_computation.1 | async-start | bytes 4194304 | tf_op jit(solution)/shard_map/all_to_all | solution.py:97
  72.7 2.0 copy.93
  76.7 2.7 fusion.61
  79.4 19.1 %all-to-all-done.1 = bf16[8,512,256]{2,1,0:T(8,128)(2,1)} async-done(((bf16[8,512,256]{2,1,0:T(8,128)(2,1)}), bf16[8,512,256]{2,1,0:T(8,128)(2,1)}, u32[]{:S(2)}, u32[]{:S(2)}) %all-to-all-start.1) | async-done | bytes 2097184 | tf_op jit(solution)/shard_map/all_to_all | solution.py:97
  98.5 2.6 fusion.60
  101.2 1.0 copy-done.8
  102.2 3.3 fusion.35
  105.5 10.2 %fusion.67 = (f32[128,8]{0,1:T(8,128)S(1)}, f32[128,8,4224]{0,2,1:T(8,128)}) fusion(f32[4224,128,8]{1,0,2:T(8,128)S(1)} %fusion.35, pred[128,4224]{0,1:T(8,128)(4,1)S(1)} %pad_add_fusion), kind=kOutput, calls=%fused_computation.126 | output fusion | flops 17305728 | bytes 35147776 | tf_op jit(solution)/shard_map/sub | solution.py:36
  115.7 7.2 %fusion.14 = bf16[128,8,4224]{0,2,1:T(8,128)(2,1)S(1)} fusion(f32[128,8,4224]{0,2,1:T(8,128)} %get-tuple-element.53, f32[128,8]{0,1:T(8,128)S(1)} %get-tuple-element.52), kind=kLoop, calls=%fused_computation.25 | loop fusion | flops 8650752 | bytes 25956352 | tf_op jit(solution)/shard_map/convert_element_type | solution.py:38
  123.0 3.4 fusion.20
  126.5 2.5 fusion.30
  129.8 7.0 %fusion.3 = bf16[128,8,4224]{0,2,1:T(8,128)(2,1)} fusion(f32[128,8]{0,1:T(8,128)S(1)} %fusion.30, f32[128,8,4224]{0,2,1:T(8,128)S(1)} %bitcast.194, f32[128,8]{0,1:T(8,128)S(1)} %get-tuple-element.52, bf16[128,128]{1,0:T(8,128)(2,1)S(1)} %get-tuple-element.44, bf16[4096,128]{1,0:T(8,128)(2,1)} %get-tuple-element.32, bf16[128,2,8,128]{0,3,2,1:T(8,128)(2,1)} %bitcast.213), kind=kOutput, calls=%fused_computation.6 | convolution fusion | flops 1126760448 | bytes 27303936 | tf_op jit(solution)/shard_map/rgd,kd->rgk/dot_general | solution.py:43
  136.8 5.9 %fusion.18 = bf16[4224,128]{1,0:T(8,128)(2,1)S(1)} fusion(bf16[128,8,4224]{0,2,1:T(8,128)(2,1)} %fusion.3, bf16[128,2,8,128]{0,3,2,1:T(8,128)(2,1)} %bitcast.209), kind=kOutput, calls=%fused_computation.36 | convolution fusion | flops 1108377600 | bytes 9994240 | tf_op jit(solution)/shard_map/rgk,rgd->kd/dot_general | solution.py:52
  143.8 1.2 slice-done.10
  145.0 1.5 pad_maximum_fusion
  146.5 4.5 %all-to-all-start.4 = ((bf16[8,512,256]{2,1,0:T(8,128)(2,1)}), bf16[8,512,256]{2,1,0:T(8,128)(2,1)}, u32[]{:S(2)}, u32[]{:S(2)}) async-start(bf16[8,512,256]{2,1,0:T(8,128)(2,1)} %pad_maximum_fusion), calls=%async_computation.4 | async-start | bytes 4194304 | tf_op jit(solution)/shard_map/all_to_all | solution.py:114
  151.0 3.3 fusion.34
  154.4 10.2 %fusion.66 = (f32[128,8]{0,1:T(8,128)S(1)}, f32[128,8,4224]{0,2,1:T(8,128)}) fusion(f32[4224,128,8]{1,0,2:T(8,128)S(1)} %fusion.34, pred[128,4224]{0,1:T(8,128)(4,1)S(1)} %pad_add_fusion), kind=kOutput, calls=%fused_computation.125 | output fusion | flops 17305728 | bytes 35147776 | tf_op jit(solution)/shard_map/sub | solution.py:36
  164.6 7.5 %fusion.15 = bf16[128,8,4224]{0,2,1:T(8,128)(2,1)S(1)} fusion(f32[128,8,4224]{0,2,1:T(8,128)} %get-tuple-element.51, f32[128,8]{0,1:T(8,128)S(1)} %get-tuple-element.50), kind=kLoop, calls=%fused_computation.26 | loop fusion | flops 8650752 | bytes 25956352 | tf_op jit(solution)/shard_map/convert_element_type | solution.py:38
  172.1 4.4 %copy-done.3 = bf16[128,8,4224]{0,2,1:T(8,128)(2,1)} copy-done((bf16[128,8,4224]{0,2,1:T(8,128)(2,1)}, bf16[128,8,4224]{0,2,1:T(8,128)(2,1)S(1)}, u32[]{:S(2)}) %copy-start.3) | copy-done | bytes 8650776
  176.5 2.5 fusion.31
  179.3 6.4 %fusion.2 = bf16[128,8,4224]{0,2,1:T(8,128)(2,1)} fusion(f32[128,8]{0,1:T(8,128)S(1)} %fusion.31, f32[128,8,4224]{0,2,1:T(8,128)S(1)} %bitcast.196, f32[128,8]{0,1:T(8,128)S(1)} %get-tuple-element.50, bf16[128,128]{1,0:T(8,128)(2,1)S(1)} %get-tuple-element.45, bf16[4096,128]{1,0:T(8,128)(2,1)} %get-tuple-element.34, bf16[128,2,8,128]{0,3,2,1:T(8,128)(2,1)S(1)} %bitcast.215), kind=kOutput, calls=%fused_computation.3 | convolution fusion | flops 1126760448 | bytes 27303936 | tf_op jit(solution)/shard_map/rgd,kd->rgk/dot_general | solution.py:43
  185.7 6.0 %fusion.19 = bf16[4224,128]{1,0:T(8,128)(2,1)S(1)} fusion(bf16[128,8,4224]{0,2,1:T(8,128)(2,1)} %fusion.2, bf16[128,2,8,128]{0,3,2,1:T(8,128)(2,1)S(1)} %bitcast.211), kind=kOutput, calls=%fused_computation.37 | convolution fusion | flops 1108377600 | bytes 9994240 | tf_op jit(solution)/shard_map/rgk,rgd->kd/dot_general | solution.py:52
  191.8 1.0 copy-done.19
  192.8 2.5 fusion.21
  195.3 1.0 copy-done.18
  196.4 1.6 pad_maximum_fusion.1
  197.9 5.7 %all-to-all-start.5 = ((bf16[8,512,256]{2,1,0:T(8,128)(2,1)}), bf16[8,512,256]{2,1,0:T(8,128)(2,1)S(1)}, u32[]{:S(2)}, u32[]{:S(2)}) async-start(bf16[8,512,256]{2,1,0:T(8,128)(2,1)} %pad_maximum_fusion.1), calls=%async_computation.5 | async-start | bytes 4194304 | tf_op jit(solution)/shard_map/all_to_all | solution.py:114
  203.7 2.0 reduce
  205.8 22.8 %all-to-all-done.5 = bf16[8,512,256]{2,1,0:T(8,128)(2,1)S(1)} async-done(((bf16[8,512,256]{2,1,0:T(8,128)(2,1)}), bf16[8,512,256]{2,1,0:T(8,128)(2,1)S(1)}, u32[]{:S(2)}, u32[]{:S(2)}) %all-to-all-start.5) | async-done | bytes 2097184 | tf_op jit(solution)/shard_map/all_to_all | solution.py:114
  229.9 10.1 %bitcast_convert_fusion = bf16[512,8192]{1,0:T(8,128)(2,1)} fusion(bf16[512,2,256]{2,0,1:T(8,128)(2,1)S(1)} %reshape.191, bf16[8192,2,256]{2,1,0:T(2,128)(2,1)} %bitcast.234), kind=kOutput, calls=%fused_computation.12 | convolution fusion | flops 4299161600 | bytes 17301504 | tf_op jit(solution)/shard_map/dot_general | solution.py:130
  240.1 4.6 %dynamic-slice_bitcast_fusion = bf16[2,128,8192]{2,1,0:T(8,128)(2,1)} fusion(bf16[2,2,128,8192]{3,2,1,0:T(8,128)(2,1)} %bitcast.197, s32[]{:T(128)S(6)} %select_n.45), kind=kLoop, calls=%fused_computation.48 | loop fusion | bytes 8388612 | tf_op jit(solution)/shard_map/jit(dynamic_index_in_dim)/squeeze | solution.py:139
  244.7 7.5 %collective-permute-done = bf16[2,128,8192]{2,1,0:T(8,128)(2,1)} collective-permute-done((bf16[2,128,8192]{2,1,0:T(8,128)(2,1)}, bf16[2,128,8192]{2,1,0:T(8,128)(2,1)}, u32[]{:S(2)}, u32[]{:S(2)}) %collective-permute-start) | collective-permute-done | bytes 4194336 | tf_op jit(solution)/shard_map/ppermute | solution.py:141
  252.2 4.9 %convert_add_fusion = f32[2,128,8192]{2,1,0:T(8,128)S(1)} fusion(bf16[2,128,8192]{2,1,0:T(8,128)(2,1)} %collective-permute-done, bf16[2,2,128,8192]{3,2,1,0:T(8,128)(2,1)} %bitcast.198, s32[]{:T(128)S(6)} %select_n.44), kind=kLoop, calls=%fused_computation.23 | loop fusion | flops 6291456 | bytes 16777220 | tf_op jit(solution)/shard_map/add | solution.py:142
  257.1 3.3 copy-done
  260.4 1.6 fusion.27
  262.0 2.0 collective-permute-start.1
  264.0 47.8 %collective-permute-done.1 = bf16[128,8192]{1,0:T(8,128)(2,1)} collective-permute-done((bf16[128,8192]{1,0:T(8,128)(2,1)}, bf16[128,8192]{1,0:T(8,128)(2,1)}, u32[]{:S(2)}, u32[]{:S(2)}) %collective-permute-start.1) | collective-permute-done | bytes 2097184 | tf_op jit(solution)/shard_map/ppermute | solution.py:146
  311.8 4.1 fusion.22
  315.9 1.1 copy-done.1
  317.0 4.7 %fusion.59 = bf16[128,8192]{1,0:T(8,128)(2,1)} fusion(f32[128]{0:T(128)S(1)} %broadcast_multiply_fusion, f32[128]{0:T(128)S(1)} %get-tuple-element.49, bf16[1,128,8192]{2,1,0:T(8,128)(2,1)S(1)} %copy-done.2, bf16[128,8192]{1,0:T(8,128)(2,1)} %collective-permute-done.1, f32[2,128,8192]{2,1,0:T(8,128)S(1)} %copy-done.1, s32[]{:T(128)S(6)} %select_n.47, ...), kind=kLoop, calls=%fused_computation.118 | loop fusion | flops 9437184 | bytes 10520068 | tf_op jit(solution)/shard_map/convert_element_type | solution.py:156
  321.8 5.0 %fusion.33 = bf16[128,1,8,128]{0,3,2,1:T(8,128)(2,1)S(1)} fusion(bf16[128,8,4224]{0,2,1:T(8,128)(2,1)} %fusion.3, bf16[128,128]{1,0:T(8,128)(2,1)S(1)} %copy-done.28, bf16[4096,128]{1,0:T(8,128)(2,1)S(1)} %copy-done.9), kind=kOutput, calls=%fused_computation.62 | convolution fusion | flops 1109721088 | bytes 9994240 | tf_op jit(solution)/shard_map/rgk,kd->rgd/dot_general | solution.py:48
  326.8 5.9 %fusion.32 = bf16[128,1,8,128]{0,3,2,1:T(8,128)(2,1)S(1)} fusion(bf16[128,8,4224]{0,2,1:T(8,128)(2,1)} %fusion.2, bf16[128,128]{1,0:T(8,128)(2,1)S(1)} %copy-done.26, bf16[4096,128]{1,0:T(8,128)(2,1)S(1)} %copy-done.7), kind=kOutput, calls=%fused_computation.61 | convolution fusion | flops 1109721088 | bytes 9994240 | tf_op jit(solution)/shard_map/rgk,kd->rgd/dot_general | solution.py:48
  335.2 4.1 all-to-all-start.6
  340.0 1.0 copy.118
  342.4 7.3 %all-to-all-done.6 = bf16[4,128,512]{2,1,0:T(8,128)(2,1)} async-done(((bf16[4,128,512]{2,1,0:T(8,128)(2,1)}), bf16[4,128,512]{2,1,0:T(8,128)(2,1)}, u32[]{:S(2)}, u32[]{:S(2)}) %all-to-all-start.6) | async-done | bytes 524320 | tf_op jit(solution)/shard_map/all_to_all | solution.py:122
  349.7 1.2 copy.112
  350.9 1.0 fusion.62
  352.0 2.0 copy.120
  354.0 2.0 copy.119
  356.1 46.6 %all-gather.3.cloned.1.call-done = bf16[512,8192]{1,0:T(8,128)(2,1)} async-done(((bf16[128,8192]{1,0:T(8,128)(2,1)}), bf16[512,8192]{1,0:T(8,128)(2,1)}) %all-gather.3.cloned.1.call-update) | async-done | bytes 8388624 | tf_op jit(solution)/shard_map/all_gather | solution.py:157
  402.7 5.6 %fusion.4 = f32[128,8192]{1,0:T(8,128)S(1)} fusion(bf16[4,128,8192]{2,1,0:T(8,128)(2,1)} %bitcast.199, pred[4]{0:T(512)(128)(4,1)S(1)} %iota_compare_fusion.3), kind=kLoop, calls=%fused_computation.11 | loop fusion | flops 11534336 | bytes 12582916 | tf_op jit(solution)/shard_map/reduce_sum | solution.py:159
  408.3 6.3 %add_bitcast_fusion = f32[1,128,8192]{2,1,0:T(8,128)} fusion(f32[128,8192]{1,0:T(8,128)S(1)} %fusion.4, f32[128]{0:T(128)S(1)} %broadcast_multiply_fusion, f32[128]{0:T(128)S(1)} %get-tuple-element.49, bf16[1,128,8192]{2,1,0:T(8,128)(2,1)S(1)} %copy-done.2, bf16[128,8192]{1,0:T(8,128)(2,1)} %collective-permute-done.1, f32[2,128,8192]{2,1,0:T(8,128)} %copy-done, ...), kind=kLoop, calls=%fused_computation.46 | loop fusion | flops 9437184 | bytes 16811524 | tf_op jit(solution)/shard_map/broadcast_in_dim | solution.py:168
  (129 shorter events, 13.9 us)
Async XLA Ops:
  10.2 12.1 %all-to-all-start.2 = ((bf16[4,128,256]{1,2,0:T(8,128)(2,1)}), bf16[4,128,256]{1,2,0:T(8,128)(2,1)S(1)}, u32[]{:S(2)}, u32[]{:S(2)}) async-start(bf16[4,128,256]{1,2,0:T(8,128)(2,1)} %maximum_bitcast_fusion.14), calls=%async_computation.2 | async-start | bytes 524288 | tf_op jit(solution)/shard_map/all_to_all | solution.py:94
  22.3 10.9 %all-to-all-start = ((bf16[4,128,256]{1,2,0:T(8,128)(2,1)}), bf16[4,128,256]{1,2,0:T(8,128)(2,1)S(1)}, u32[]{:S(2)}, u32[]{:S(2)}) async-start(bf16[4,128,256]{1,2,0:T(8,128)(2,1)} %maximum_bitcast_fusion.13), calls=%async_computation | async-start | bytes 524288 | tf_op jit(solution)/shard_map/all_to_all | solution.py:94
  25.7 15.7 %copy-start.32 = (s32[1,128]{1,0:T(1,128)S(1)}, s32[1,128]{1,0:T(1,128)}, u32[]{:S(2)}) copy-start(s32[1,128]{1,0:T(1,128)} %param.21) | copy-start | bytes 1540
  25.7 15.7 %copy-start.34 = (s32[1,2]{1,0:T(1,128)S(1)}, s32[1,2]{1,0:T(1,128)}, u32[]{:S(2)}) copy-start(s32[1,2]{1,0:T(1,128)} %param.22) | copy-start | bytes 28
  25.7 15.8 %copy-start.33 = (s32[3,16]{1,0:T(4,128)S(1)}, s32[3,16]{1,0:T(4,128)}, u32[]{:S(2)}) copy-start(s32[3,16]{1,0:T(4,128)} %param.23) | copy-start | bytes 580
  25.7 15.9 %copy-start.29 = (bf16[1,128,256]{2,1,0:T(8,128)(2,1)S(1)}, bf16[1,128,256]{2,1,0:T(8,128)(2,1)}, u32[]{:S(2)}) copy-start(bf16[1,128,256]{2,1,0:T(8,128)(2,1)} %param.13) | copy-start | bytes 196612
  34.6 32.1 %all-to-all-start.3 = ((bf16[8,512,256]{2,1,0:T(8,128)(2,1)}), bf16[8,512,256]{2,1,0:T(8,128)(2,1)S(1)}, u32[]{:S(2)}, u32[]{:S(2)}) async-start(bf16[8,512,256]{2,1,0:T(8,128)(2,1)} %broadcast_in_dim.95), calls=%async_computation.3 | async-start | bytes 4194304 | tf_op jit(solution)/shard_map/all_to_all | solution.py:97
  41.4 33.4 %copy-start.14 = (bf16[1,128,2048]{1,2,0:T(8,128)(2,1)}, bf16[1,128,2048]{1,2,0:T(8,128)(2,1)S(1)}, u32[]{:S(2)}) copy-start(bf16[1,128,2048]{1,2,0:T(8,128)(2,1)S(1)} %copy.95) | copy-start | bytes 1572868
  43.2 31.6 %copy-start.20 = (bf16[128,1,8,128]{0,3,2,1:T(8,128)(2,1)S(1)}, bf16[128,1,8,128]{0,3,2,1:T(8,128)(2,1)}, u32[]{:S(2)}) copy-start(bf16[128,1,8,128]{0,3,2,1:T(8,128)(2,1)} %get-tuple-element.38) | copy-start | bytes 786436
  66.7 9.8 %copy-start.5 = (bf16[8,512,256]{2,1,0:T(8,128)(2,1)}, bf16[8,512,256]{2,1,0:T(8,128)(2,1)S(1)}, u32[]{:S(2)}) copy-start(bf16[8,512,256]{2,1,0:T(8,128)(2,1)S(1)} %all-to-all-done.3) | copy-start | bytes 6291460
  66.7 9.8 %copy-start.30 = (bf16[1,128,256]{2,1,0:T(8,128)(2,1)S(1)}, bf16[1,128,256]{2,1,0:T(8,128)(2,1)}, u32[]{:S(2)}) copy-start(bf16[1,128,256]{2,1,0:T(8,128)(2,1)} %param.14) | copy-start | bytes 196612
  68.3 30.2 %all-to-all-start.1 = ((bf16[8,512,256]{2,1,0:T(8,128)(2,1)}), bf16[8,512,256]{2,1,0:T(8,128)(2,1)}, u32[]{:S(2)}, u32[]{:S(2)}) async-start(bf16[8,512,256]{2,1,0:T(8,128)(2,1)} %broadcast_in_dim.92), calls=%async_computation.1 | async-start | bytes 4194304 | tf_op jit(solution)/shard_map/all_to_all | solution.py:97
  76.7 25.4 %copy-start.27 = (bf16[128,128]{1,0:T(8,128)(2,1)S(1)}, bf16[128,128]{1,0:T(8,128)(2,1)}, u32[]{:S(2)}) copy-start(bf16[128,128]{1,0:T(8,128)(2,1)} %get-tuple-element.46) | copy-start | bytes 98308
  79.4 71.6 %copy-start.6 = (bf16[4096,128]{1,0:T(8,128)(2,1)}, bf16[4096,128]{1,0:T(8,128)(2,1)S(1)}, u32[]{:S(2)}) copy-start(bf16[4096,128]{1,0:T(8,128)(2,1)S(1)} %get-tuple-element.35) | copy-start | bytes 3145732
  101.1 1.0 copy-start.8
  115.7 7.2 %copy-start.15 = (bf16[1,128,2048]{1,2,0:T(8,128)(2,1)S(1)}, bf16[1,128,2048]{1,2,0:T(8,128)(2,1)}, u32[]{:S(2)}) copy-start(bf16[1,128,2048]{1,2,0:T(8,128)(2,1)} %copy-done.14) | copy-start | bytes 1572868
  123.0 3.5 copy-start.22
  123.0 3.5 copy-start.24
  123.0 6.0 %slice-start = ((s8[17301504]{0:T(1024)(128)(4,1)}), s8[4194304]{0:T(1024)(128)(4,1)S(1)}, s32[]{:S(2)}) async-start(s8[17301504]{0:T(1024)(128)(4,1)} %bitcast.193), calls=%async_computation.8 | async-start | bytes 8388608
  123.0 6.0 %slice-start.1 = ((s8[17301504]{0:T(1024)(128)(4,1)}), s8[4194304]{0:T(1024)(128)(4,1)S(1)}, s32[]{:S(2)}) async-start(s8[17301504]{0:T(1024)(128)(4,1)} %bitcast.193), calls=%async_computation.9 | async-start | bytes 8388608
  123.0 6.0 %slice-start.2 = ((s8[17301504]{0:T(1024)(128)(4,1)}), s8[4194304]{0:T(1024)(128)(4,1)S(1)}, s32[]{:S(2)}) async-start(s8[17301504]{0:T(1024)(128)(4,1)} %bitcast.193), calls=%async_computation.10 | async-start | bytes 8388608
  126.5 3.4 slice-start.3
  126.5 3.4 slice-start.4
  142.7 1.0 copy-start.17
  143.7 1.2 slice-start.10
  144.9 6.1 %copy-start.25 = (bf16[128,128]{1,0:T(8,128)(2,1)S(1)}, bf16[128,128]{1,0:T(8,128)(2,1)}, u32[]{:S(2)}) copy-start(bf16[128,128]{1,0:T(8,128)(2,1)} %get-tuple-element.47) | copy-start | bytes 98308
  146.5 51.4 %all-to-all-start.4 = ((bf16[8,512,256]{2,1,0:T(8,128)(2,1)}), bf16[8,512,256]{2,1,0:T(8,128)(2,1)}, u32[]{:S(2)}, u32[]{:S(2)}) async-start(bf16[8,512,256]{2,1,0:T(8,128)(2,1)} %pad_maximum_fusion), calls=%async_computation.4 | async-start | bytes 4194304 | tf_op jit(solution)/shard_map/all_to_all | solution.py:114
  164.6 11.9 %copy-start.21 = (bf16[4096,128]{1,0:T(8,128)(2,1)S(1)}, bf16[4096,128]{1,0:T(8,128)(2,1)}, u32[]{:S(2)}) copy-start(bf16[4096,128]{1,0:T(8,128)(2,1)} %get-tuple-element.34) | copy-start | bytes 3145732
  164.6 11.9 %copy-start.23 = (bf16[128,1,8,128]{3,0,2,1:T(8,128)(2,1)S(1)}, bf16[128,1,8,128]{3,0,2,1:T(8,128)(2,1)}, u32[]{:S(2)}) copy-start(bf16[128,1,8,128]{3,0,2,1:T(8,128)(2,1)} %copy.140) | copy-start | bytes 786436
  164.6 14.4 %slice-start.5 = ((s8[17301504]{0:T(1024)(128)(4,1)}), s8[4194304]{0:T(1024)(128)(4,1)S(1)}, s32[]{:S(2)}) async-start(s8[17301504]{0:T(1024)(128)(4,1)} %bitcast.195), calls=%async_computation.13 | async-start | bytes 8388608
  164.6 14.4 %slice-start.6 = ((s8[17301504]{0:T(1024)(128)(4,1)}), s8[4194304]{0:T(1024)(128)(4,1)S(1)}, s32[]{:S(2)}) async-start(s8[17301504]{0:T(1024)(128)(4,1)} %bitcast.195), calls=%async_computation.14 | async-start | bytes 8388608
  164.6 14.4 %slice-start.7 = ((s8[17301504]{0:T(1024)(128)(4,1)}), s8[4194304]{0:T(1024)(128)(4,1)S(1)}, s32[]{:S(2)}) async-start(s8[17301504]{0:T(1024)(128)(4,1)} %bitcast.195), calls=%async_computation.15 | async-start | bytes 8388608
  164.6 14.4 %slice-start.8 = ((s8[17301504]{0:T(1024)(128)(4,1)}), s8[4194304]{0:T(1024)(128)(4,1)S(1)}, s32[]{:S(2)}) async-start(s8[17301504]{0:T(1024)(128)(4,1)} %bitcast.195), calls=%async_computation.16 | async-start | bytes 8388608
  172.1 4.4 %copy-start.3 = (bf16[128,8,4224]{0,2,1:T(8,128)(2,1)}, bf16[128,8,4224]{0,2,1:T(8,128)(2,1)S(1)}, u32[]{:S(2)}) copy-start(bf16[128,8,4224]{0,2,1:T(8,128)(2,1)S(1)} %fusion.15) | copy-start | bytes 25952260
  176.5 2.7 slice-start.9
  176.5 2.8 copy-start.16
  179.3 6.4 %copy-start.13 = (bf16[1,128,2048]{1,2,0:T(8,128)(2,1)S(1)}, bf16[1,128,2048]{1,2,0:T(8,128)(2,1)}, u32[]{:S(2)}) copy-start(bf16[1,128,2048]{1,2,0:T(8,128)(2,1)} %copy.93) | copy-start | bytes 1572868
  185.7 7.1 %copy-start.4 = (bf16[128,8,4224]{0,2,1:T(8,128)(2,1)S(1)}, bf16[128,8,4224]{0,2,1:T(8,128)(2,1)}, u32[]{:S(2)}) copy-start(bf16[128,8,4224]{0,2,1:T(8,128)(2,1)} %copy-done.3) | copy-start | bytes 25952260
  191.7 1.0 copy-start.19
  195.3 1.0 copy-start.18
  197.9 30.6 %all-to-all-start.5 = ((bf16[8,512,256]{2,1,0:T(8,128)(2,1)}), bf16[8,512,256]{2,1,0:T(8,128)(2,1)S(1)}, u32[]{:S(2)}, u32[]{:S(2)}) async-start(bf16[8,512,256]{2,1,0:T(8,128)(2,1)} %pad_maximum_fusion.1), calls=%async_computation.5 | async-start | bytes 4194304 | tf_op jit(solution)/shard_map/all_to_all | solution.py:114
  203.6 199.1 %all-gather.3.cloned.1.call-start = ((), (), s32[]{:S(2)}) async-start(), calls=%async_computation.7 | async-start | bytes 10485760 | tf_op jit(solution)/shard_map/all_gather | solution.py:157
  229.0 11.1 %copy-start.11 = (bf16[512,256]{1,0:T(8,128)(2,1)}, bf16[512,256]{1,0:T(8,128)(2,1)S(1)}, u32[]{:S(2)}) copy-start(bf16[512,256]{1,0:T(8,128)(2,1)S(1)} %reduce.1) | copy-start | bytes 786436
  244.7 7.5 %collective-permute-start = (bf16[2,128,8192]{2,1,0:T(8,128)(2,1)}, bf16[2,128,8192]{2,1,0:T(8,128)(2,1)}, u32[]{:S(2)}, u32[]{:S(2)}) collective-permute-start(bf16[2,128,8192]{2,1,0:T(8,128)(2,1)} %dynamic-slice_bitcast_fusion), channel_id=1, source_target_pairs={{0,1},{1,0},{2,3},{3,2},{4,5},{5,4},{6,7},{7,6},{8,9},{9,8},{10,11... | collective-permute-start | bytes 12582920 | tf_op jit(solution)/shard_map/ppermute | solution.py:141
  257.1 3.3 copy-start
  260.4 3.5 copy-start.31
  260.4 51.4 %copy-start.2 = (bf16[1,128,8192]{2,1,0:T(8,128)(2,1)S(1)}, bf16[1,128,8192]{2,1,0:T(8,128)(2,1)}, u32[]{:S(2)}) copy-start(bf16[1,128,8192]{2,1,0:T(8,128)(2,1)} %param.19) | copy-start | bytes 6291460
  262.0 49.8 %collective-permute-start.1 = (bf16[128,8192]{1,0:T(8,128)(2,1)}, bf16[128,8192]{1,0:T(8,128)(2,1)}, u32[]{:S(2)}, u32[]{:S(2)}) collective-permute-start(bf16[128,8192]{1,0:T(8,128)(2,1)} %fusion.27), channel_id=1, source_target_pairs={{0,2},{1,3},{2,0},{3,1},{4,6},{5,7},{6,4},{7,5},{8,10},{9,11},{10,... | collective-permute-start | bytes 6291464 | tf_op jit(solution)/shard_map/ppermute | solution.py:146
  311.8 5.2 %copy-start.1 = (f32[2,128,8192]{2,1,0:T(8,128)S(1)}, f32[2,128,8192]{2,1,0:T(8,128)}, u32[]{:S(2)}) copy-start(f32[2,128,8192]{2,1,0:T(8,128)} %copy-done) | copy-start | bytes 25165828
  317.0 4.8 %copy-start.9 = (bf16[4096,128]{1,0:T(8,128)(2,1)S(1)}, bf16[4096,128]{1,0:T(8,128)(2,1)}, u32[]{:S(2)}) copy-start(bf16[4096,128]{1,0:T(8,128)(2,1)} %copy-done.8) | copy-start | bytes 3145732
  317.0 4.8 %copy-start.28 = (bf16[128,128]{1,0:T(8,128)(2,1)S(1)}, bf16[128,128]{1,0:T(8,128)(2,1)}, u32[]{:S(2)}) copy-start(bf16[128,128]{1,0:T(8,128)(2,1)} %get-tuple-element.46) | copy-start | bytes 98308
  321.8 5.0 %copy-start.7 = (bf16[4096,128]{1,0:T(8,128)(2,1)S(1)}, bf16[4096,128]{1,0:T(8,128)(2,1)}, u32[]{:S(2)}) copy-start(bf16[4096,128]{1,0:T(8,128)(2,1)} %copy-done.6) | copy-start | bytes 3145732
  321.8 5.0 %copy-start.26 = (bf16[128,128]{1,0:T(8,128)(2,1)S(1)}, bf16[128,128]{1,0:T(8,128)(2,1)}, u32[]{:S(2)}) copy-start(bf16[128,128]{1,0:T(8,128)(2,1)} %get-tuple-element.47) | copy-start | bytes 98308
  326.8 6.8 %copy-start.10 = (bf16[4224,128]{1,0:T(8,128)(2,1)S(1)}, bf16[4224,128]{1,0:T(8,128)(2,1)}, u32[]{:S(2)}) copy-start(bf16[4224,128]{1,0:T(8,128)(2,1)} %fusion.20) | copy-start | bytes 3244036
  326.8 7.5 %copy-start.12 = (bf16[512,256]{1,0:T(8,128)(2,1)S(1)}, bf16[512,256]{1,0:T(8,128)(2,1)}, u32[]{:S(2)}) copy-start(bf16[512,256]{1,0:T(8,128)(2,1)} %copy-done.11) | copy-start | bytes 786436
  335.2 14.5 %all-to-all-start.6 = ((bf16[4,128,512]{2,1,0:T(8,128)(2,1)}), bf16[4,128,512]{2,1,0:T(8,128)(2,1)}, u32[]{:S(2)}, u32[]{:S(2)}) async-start(bf16[4,128,512]{2,1,0:T(8,128)(2,1)} %pad_maximum_fusion.3), calls=%async_computation.6 | async-start | bytes 1048576 | tf_op jit(solution)/shard_map/all_to_all | solution.py:122
Sparse Core Ops, SparseCore 0:
  321.8 80.7 all-gather.2
